TPU v7x, 256 devices: a whole 4x4x8 slice. The times are simulated.
256 devices in a mesh: blk: 128 (over x, z, y_hi, core), grp: 2 (over y_lo).
Axes of the slice: x: 4, y: 4 (y_hi: 2, y_lo: 2; y = y_hi * 2 + y_lo), z: 8, core: 2. Of those that a mesh axis runs over, the one named last changes fastest.
Arguments:
- raw: bfloat16 [32, 8192, 2400], P(None, ('blk', 'grp')), may hold values from -1200 to 1200
- partner: int32 [3, 128], replicated, may hold values from 0 to 127, as said below
Outputs:
- cross: bfloat16 [3, 256, 8192, 128], P(None, 'grp', 'blk')
Inputs may be any that keep to these rules, and one draw needn't show every extreme that they name: Each row pairs off the 128 blocks: no block is its own partner, and the partner of a block's partner is the block itself. No two rows are equal.
All inputs are finite; a program needn't handle non-finite values.
Results may differ from a plain program's by a relative error of at most 0.0065.
Values may be sent and summed in bfloat16 or wider, within the bound.
No kernel may reach another device: no remote copies, remote signals or barrier semaphores. Data moves between devices by JAX's collectives and lax.ppermute only.
A program may use at most 128 MiB of HBM per device.

v0:
```python
import math

import jax
import jax.numpy as jnp
from jax import lax
from jax.sharding import PartitionSpec as P

F = 256


first_bin = 8
epsilon = 1e-06


def dft_table(length, num_bins):
    sample_idx = lax.broadcasted_iota(jnp.int32, (length, num_bins), 0)
    bin_index = lax.broadcasted_iota(jnp.int32, (length, num_bins), 1) + first_bin
    phase_angle = (sample_idx * bin_index % length).astype(jnp.float32) * (2.0 * math.pi / length)
    return jnp.concatenate([jnp.cos(phase_angle), -jnp.sin(phase_angle)], axis=1).astype(
        jnp.bfloat16
    )


def whiten(samples, num_bins):
    seg_count, chan_count, length = samples.shape
    spectrum = jnp.dot(
        samples.reshape(seg_count * chan_count, length),
        dft_table(length, num_bins),
        preferred_element_type=jnp.float32,
    ).reshape(seg_count, chan_count, 2 * num_bins)
    real_part = spectrum[:, :, :num_bins]
    imag_part = spectrum[:, :, num_bins:]
    bin_power = jnp.mean(real_part * real_part + imag_part * imag_part, axis=0)
    factor = lax.rsqrt(bin_power + epsilon)
    joined = jnp.concatenate([real_part * factor, imag_part * factor], axis=0)
    return jnp.transpose(joined, (2, 1, 0)).astype(jnp.bfloat16)


def per_device(raw, partner):
    spectra = whiten(raw, F)
    halves = lax.all_to_all(spectra, "grp", split_axis=0, concat_axis=1, tiled=True)
    owned = lax.all_to_all(halves[:, None], "blk", split_axis=0, concat_axis=1, tiled=True)
    seg_count = owned.shape[-1] // 2
    norm_scale = 1.0 / math.sqrt(seg_count)
    gathered = jnp.transpose(jnp.take(owned, partner, axis=1), (1, 2, 0, 3, 4))
    other = lax.all_to_all(gathered, "blk", split_axis=1, concat_axis=2, tiled=True)[:, 0]
    turned = jnp.concatenate([-other[..., seg_count:], other[..., :seg_count]], axis=-1)
    both = jnp.concatenate([other, turned], axis=2)
    result = jnp.einsum("fcs,rfjs->rfcj", halves, both, preferred_element_type=jnp.float32)
    return (result * norm_scale).astype(jnp.bfloat16)


def solution(mesh):
    placed = (P(None, ("blk", "grp"), None), P())
    return jax.shard_map(
        per_device,
        mesh=mesh,
        in_specs=placed,
        out_specs=P(None, "grp", "blk", None),
        check_vma=False,
    )
```

profile of v0, /device:TPU:32, one launch (start us, length us, event | category | flops | bytes accessed | tf_op | source)
XLA Modules:
  0.0 261.2 jit_solution(16226962387855263541)
XLA Ops:
  0.0 10.4 %cosine_convert_fusion = (bf16[2400,256]{1,0:T(8,128)(2,1)S(1)}, bf16[2400,256]{1,0:T(8,128)(2,1)S(1)}) fusion(s32[256]{0:T(256)S(1)} %iota_add_fusion), kind=kLoop, calls=%fused_computation.19 | loop fusion | flops 7372800 | bytes 2458624 | tf_op jit(solution)/shard_map/convert.2
  10.4 6.7 %fusion.18 = f32[1024,512]{0,1:T(8,128)} fusion(bf16[1024,2400]{1,0:T(8,128)(2,1)} %bitcast.37, bf16[2400,256]{1,0:T(8,128)(2,1)S(1)} %get-tuple-element.10, bf16[2400,256]{1,0:T(8,128)(2,1)S(1)} %get-tuple-element.9), kind=kOutput, calls=%fused_computation.24 | convolution fusion | flops 2521497600 | bytes 9469952 | tf_op jit(solution)/shard_map/dot_general | solution.py:26
  17.1 1.9 copy.23
  19.2 0.3 multiply_convert_fusion.2
  19.6 3.6 %copy.24 = bf16[256,32,64]{2,1,0:T(8,128)(2,1)S(1)} copy(bf16[256,32,64]{0,1,2:T(8,128)(2,1)S(1)} %maximum_bitcast_fusion) | data formatting | bytes 2097152 | tf_op jit(solution)/shard_map/convert_element_type | solution.py:36
  23.1 1.6 reshape.54
  24.8 16.3 %all_to_all.39 = bf16[2,2,131072]{2,1,0:T(2,128)(2,1)S(1)} all-to-all(bf16[2,2,131072]{2,1,0:T(2,128)(2,1)S(1)} %reshape.54), channel_id=1, replica_groups=mesh['blk'=128,'grp'=2] {'grp'}, dimensions={0} | all-to-all | bytes 2097152 | tf_op jit(solution)/shard_map/all_to_all | solution.py:41
  41.1 2.3 reshape.55
  43.4 2.3 copy.25
  45.7 2.3 reshape.56
  48.0 15.0 %all-to-all-start.1 = ((bf16[128,2,2048]{2,1,0:T(2,128)(2,1)}), bf16[128,2,2048]{2,1,0:T(2,128)(2,1)S(1)}, u32[]{:S(2)}, u32[]{:S(2)}) async-start(bf16[128,2,2048]{2,1,0:T(2,128)(2,1)} %reshape.56), calls=%async_computation.1 | async-start | bytes 2097152 | tf_op jit(solution)/shard_map/all_to_all | solution.py:42
  63.1 30.9 %all-to-all-done.1 = bf16[128,2,2048]{2,1,0:T(2,128)(2,1)S(1)} async-done(((bf16[128,2,2048]{2,1,0:T(2,128)(2,1)}), bf16[128,2,2048]{2,1,0:T(2,128)(2,1)S(1)}, u32[]{:S(2)}, u32[]{:S(2)}) %all-to-all-start.1) | async-done | bytes 1048608 | tf_op jit(solution)/shard_map/all_to_all | solution.py:42
  94.0 1.4 reshape.57
  95.3 13.3 %gather_fusion = bf16[384,64,64]{2,1,0:T(8,128)(2,1)} fusion(bf16[128,64,64]{2,1,0:T(8,128)(2,1)S(1)} %bitcast.29, s32[1024]{0:T(1024)S(1)} %pad_clamp_fusion), kind=kCustom, calls=%fused_computation | custom fusion | bytes 6292992 | tf_op jit(solution)/shard_map/jit(_take)/gather | solution.py:45
  108.7 9.8 %copy.30 = bf16[3,128,1,64,64]{1,0,4,3,2:T(4,128)(2,1)} copy(bf16[3,128,1,64,64]{4,3,1,0,2:T(8,128)(2,1)} %bitcast.31) | data formatting | bytes 6291456 | tf_op jit(solution)/shard_map/jit(_take)/gather | solution.py:45
  118.5 5.9 %broadcast_select_fusion = bf16[3,128,1,64,64]{1,0,4,3,2:T(4,128)(2,1)} fusion(bf16[3,128,1,64,64]{1,0,4,3,2:T(4,128)(2,1)} %copy.30, pred[3,128]{1,0:T(4,128)(4,1)S(1)} %compare_and_fusion), kind=kLoop, calls=%fused_computation.9 | loop fusion | flops 1572864 | bytes 6291840 | tf_op jit(solution)/shard_map/jit(_take)/select_n | solution.py:45
  124.4 9.8 %copy.27 = bf16[3,128,1,64,64]{3,4,0,2,1:T(8,128)(2,1)} copy(bf16[3,128,1,64,64]{1,0,4,3,2:T(4,128)(2,1)} %broadcast_select_fusion) | data formatting | bytes 6291456 | tf_op jit(solution)/shard_map/jit(_take)/select_n | solution.py:45
  134.3 9.7 %reshape.58 = bf16[128,2,6144]{2,1,0:T(2,128)(2,1)S(1)} reshape(bf16[128,1,3,64,64]{4,3,2,1,0:T(8,128)(2,1)} %bitcast.30) | data formatting | bytes 6291456
  144.0 82.7 %all_to_all.40 = bf16[128,2,6144]{2,1,0:T(2,128)(2,1)} all-to-all(bf16[128,2,6144]{2,1,0:T(2,128)(2,1)S(1)} %reshape.58), channel_id=1, replica_groups=mesh['blk'=128,'grp'=2] {'blk'}, dimensions={0} | all-to-all | bytes 6291456 | tf_op jit(solution)/shard_map/all_to_all | solution.py:46
  226.6 11.1 %reshape.59 = bf16[128,1,3,64,64]{4,3,2,1,0:T(8,128)(2,1)} reshape(bf16[128,2,6144]{2,1,0:T(2,128)(2,1)} %all_to_all.40) | data formatting | bytes 6291456
  237.7 4.3 %bitcast_bitcast_fusion = bf16[3,128,64,64]{2,3,0,1:T(8,128)(2,1)S(1)} fusion(bf16[128,1,3,64,64]{4,3,2,1,0:T(8,128)(2,1)} %reshape.59), kind=kLoop, calls=%fused_computation.37 | loop fusion | bytes 6291456 | tf_op jit(solution)/shard_map/squeeze | solution.py:46
  242.0 3.3 %slice_negate_fusion = (bf16[3,128,64,32]{2,3,0,1:T(8,128)(2,1)}, bf16[3,128,64,32]{2,3,0,1:T(8,128)(2,1)}) fusion(bf16[3,128,64,64]{2,3,0,1:T(8,128)(2,1)S(1)} %bitcast_bitcast_fusion), kind=kLoop, calls=%fused_computation.11 | loop fusion | flops 786432 | bytes 6291456 | tf_op jit(solution)/shard_map/neg | solution.py:47
  245.3 8.5 %fusion = bf16[3,128,64,128]{3,2,0,1:T(8,128)(2,1)} fusion(bf16[128,64,64,1]{2,1,3,0:T(8,128)(2,1)S(1)} %bitcast.35, bf16[3,128,64,32]{2,3,0,1:T(8,128)(2,1)} %get-tuple-element.6, bf16[3,128,64,32]{2,3,0,1:T(8,128)(2,1)} %get-tuple-element.5, bf16[3,128,64,64]{2,3,0,1:T(8,128)(2,1)S(1)} %bitcast_bitcast_fusion), kind=kOutput, calls=%fused_computation.2 | convolution fusion | flops 427819008 | bytes 13631488 | tf_op jit(solution)/shard_map/fcs,rfjs->rfcj/dot_general | solution.py:49
  253.7 7.5 %copy.28 = bf16[3,128,64,128]{3,2,1,0:T(8,128)(2,1)} copy(bf16[3,128,64,128]{3,2,0,1:T(8,128)(2,1)} %fusion) | data formatting | bytes 12582912 | tf_op jit(solution)/shard_map/convert_element_type | solution.py:50
  (13 shorter events, 0.3 us)
Async XLA Ops:
  45.7 17.4 %copy-start = (bf16[2,128,32,64]{3,2,0,1:T(8,128)(2,1)}, bf16[2,128,32,64]{3,2,0,1:T(8,128)(2,1)S(1)}, u32[]{:S(2)}) copy-start(bf16[2,128,32,64]{3,2,0,1:T(8,128)(2,1)S(1)} %copy.25) | copy-start | bytes 3145732
  45.7 17.3 %copy-start.2 = (s32[3,128]{1,0:T(4,128)S(1)}, s32[3,128]{1,0:T(4,128)}, u32[]{:S(2)}) copy-start(s32[3,128]{1,0:T(4,128)} %param.3) | copy-start | bytes 4612
  48.0 46.0 %all-to-all-start.1 = ((bf16[128,2,2048]{2,1,0:T(2,128)(2,1)}), bf16[128,2,2048]{2,1,0:T(2,128)(2,1)S(1)}, u32[]{:S(2)}, u32[]{:S(2)}) async-start(bf16[128,2,2048]{2,1,0:T(2,128)(2,1)} %reshape.56), calls=%async_computation.1 | async-start | bytes 2097152 | tf_op jit(solution)/shard_map/all_to_all | solution.py:42
  242.0 3.3 %copy-start.1 = (bf16[2,128,32,64]{3,2,0,1:T(8,128)(2,1)S(1)}, bf16[2,128,32,64]{3,2,0,1:T(8,128)(2,1)}, u32[]{:S(2)}) copy-start(bf16[2,128,32,64]{3,2,0,1:T(8,128)(2,1)} %copy-done) | copy-start | bytes 3145732
where the time goes:
time: 262 us; the launch traced here: 261 us
  blocking collectives  99 us (38%)
  local copies, waits for them, and re-layouts  80.9 us (31%)
  waiting for transfers between devices  30.9 us (12%)
  other arithmetic  20.1 us (8%)
  matrix products  15.2 us (6%)
  starting transfers between devices  15 us (6%)
    all_to_all x1, blocking collectives, per_device(): lax.all_to_all(gathered, 'blk', split_axis=1, concat_axis=2, tiled=True)  82.7 us
    all_to_all x1, waiting for transfers between devices, per_device(): lax.all_to_all(halves[:, None], 'blk', split_axis=0, concat_axis=1, tiled...  30.9 us
    unnamed x12, local copies, waits for them, and re-layouts  28.4 us
    gather x2, local copies, waits for them, and re-layouts, per_device(): gathered = jnp.transpose(jnp.take(owned, partner, axis=1), (1, 2, 0, 3, 4))  23.2 us
    all_to_all x1, blocking collectives, per_device(): lax.all_to_all(spectra, 'grp', split_axis=0, concat_axis=1, tiled=True)  16.3 us
    all_to_all x1, starting transfers between devices, per_device(): lax.all_to_all(halves[:, None], 'blk', split_axis=0, concat_axis=1, tiled...  15 us
    another operation x2, other arithmetic  10.6 us
    select_n x1, local copies, waits for them, and re-layouts, per_device(): gathered = jnp.transpose(jnp.take(owned, partner, axis=1), (1, 2, 0, 3, 4))  9.81 us
  transfers between devices with their start and end apart: 1, of which 1 were waited for; matrix products, arithmetic and copies ran while one was open for 0% of the time, Pallas kernels for 0%

commit v1 on v0

--- a/solution.py
+++ b/solution.py
@@ -12,13 +12,21 @@
 epsilon = 1e-06
 
 
+def phase_table(step, rows, num_bins, length):
+    sample_idx = lax.broadcasted_iota(jnp.int32, (rows, num_bins), 0) * step
+    bin_index = lax.broadcasted_iota(jnp.int32, (rows, num_bins), 1) + first_bin
+    phase_angle = (sample_idx * bin_index % length).astype(jnp.float32) * (2.0 * math.pi / length)
+    return jnp.cos(phase_angle), jnp.sin(phase_angle)
+
+
 def dft_table(length, num_bins):
-    sample_idx = lax.broadcasted_iota(jnp.int32, (length, num_bins), 0)
-    bin_index = lax.broadcasted_iota(jnp.int32, (length, num_bins), 1) + first_bin
-    phase_angle = (sample_idx * bin_index % length).astype(jnp.float32) * (2.0 * math.pi / length)
-    return jnp.concatenate([jnp.cos(phase_angle), -jnp.sin(phase_angle)], axis=1).astype(
-        jnp.bfloat16
-    )
+    step = 48 if length % 48 == 0 else 1
+    cos_c, sin_c = phase_table(step, length // step, num_bins, length)
+    cos_f, sin_f = phase_table(1, step, num_bins, length)
+    cos_t = cos_c[:, None] * cos_f[None] - sin_c[:, None] * sin_f[None]
+    sin_t = sin_c[:, None] * cos_f[None] + cos_c[:, None] * sin_f[None]
+    table = jnp.concatenate([cos_t, -sin_t], axis=-1).reshape(length, 2 * num_bins)
+    return table.astype(jnp.bfloat16)
 
 
 def whiten(samples, num_bins):
@@ -37,16 +45,31 @@
 
 
 def per_device(raw, partner):
+    n_blk = lax.axis_size("blk")
     spectra = whiten(raw, F)
-    halves = lax.all_to_all(spectra, "grp", split_axis=0, concat_axis=1, tiled=True)
-    owned = lax.all_to_all(halves[:, None], "blk", split_axis=0, concat_axis=1, tiled=True)
-    seg_count = owned.shape[-1] // 2
+    n_bin, half_ch, two_seg = spectra.shape
+    seg_count = two_seg // 2
     norm_scale = 1.0 / math.sqrt(seg_count)
-    gathered = jnp.transpose(jnp.take(owned, partner, axis=1), (1, 2, 0, 3, 4))
-    other = lax.all_to_all(gathered, "blk", split_axis=1, concat_axis=2, tiled=True)[:, 0]
+    halves = lax.all_to_all(
+        spectra.reshape(n_bin, half_ch * two_seg), "grp", split_axis=0, concat_axis=1, tiled=True
+    )
+    own_bins, record = halves.shape
+    per_owner = own_bins // n_blk
+    owned = lax.all_to_all(
+        halves.reshape(n_blk, per_owner * record), "blk", split_axis=0, concat_axis=0, tiled=True
+    )
+    rounds = partner.shape[0]
+    gathered = jnp.take(owned, partner.reshape(-1), axis=0, mode="clip")
+    gathered = jnp.transpose(gathered.reshape(rounds, n_blk, per_owner * record), (1, 0, 2))
+    other = lax.all_to_all(gathered, "blk", split_axis=0, concat_axis=0, tiled=True)
+    block_ch = record // two_seg
+    other = other.reshape(n_blk, rounds, per_owner, block_ch, two_seg)
+    other = jnp.transpose(other, (1, 0, 2, 3, 4)).reshape(rounds, own_bins, block_ch, two_seg)
+
+    own = halves.reshape(own_bins, block_ch, two_seg)
     turned = jnp.concatenate([-other[..., seg_count:], other[..., :seg_count]], axis=-1)
     both = jnp.concatenate([other, turned], axis=2)
-    result = jnp.einsum("fcs,rfjs->rfcj", halves, both, preferred_element_type=jnp.float32)
+    result = jnp.einsum("fcs,rfjs->rfcj", own, both, preferred_element_type=jnp.float32)
     return (result * norm_scale).astype(jnp.bfloat16)
 
 

time: 262 us -> 243 us (0.927)
  waiting for transfers between devices: 30.9 us -> 125 us
  blocking collectives: 99 us -> 16.3 us
  local copies, waits for them, and re-layouts: 80.9 us -> 50.9 us
  other arithmetic: 20.1 us -> 9.02 us
  starting transfers between devices: 15 us -> 22.5 us
    all_to_all x1 -> x2, waiting for transfers between devices: 30.9 us -> 125 us  [the longest x1 94 us: per_device(): lax.all_to_all(gathered, 'blk', split_axis=0, concat_axis=0, tiled=True)]
    all_to_all x2 -> x1, blocking collectives: 99 us -> 16.3 us  [per_device(): lax.all_to_all(spectra.reshape(n_bin, half_ch * two_seg), 'grp', split_ax...]
    reshape x0 -> x3, local copies, waits for them, and re-layouts: none -> 21.6 us  [the longest x1 11.2 us: per_device(): other = other.reshape(n_blk, rounds, per_owner, block_ch, two_seg)]
    unnamed x12 -> x8, local copies, waits for them, and re-layouts: 28.4 us -> 8.29 us
    gather x2 -> x1, local copies, waits for them, and re-layouts: 23.2 us -> 4.05 us  [per_device(): gathered = jnp.take(owned, partner.reshape(-1), axis=0, mode='clip')]
    select_n x1 -> x0, local copies, waits for them, and re-layouts: 9.81 us -> none  [per_device(): gathered = jnp.transpose(jnp.take(owned, partner, axis=1), (1, 2, 0, 3, 4))]
    another operation x2, other arithmetic: 10.6 us -> 1.44 us
    all_to_all x1 -> x2, starting transfers between devices: 15 us -> 22.5 us  [the longest x1 15 us: per_device(): lax.all_to_all(halves.reshape(n_blk, per_owner * record), 'blk', split_ax...]
  transfers between devices with their start and end apart: 1 -> 2, of which waited for: 1 -> 2; matrix products, arithmetic and copies ran while one was open for 0% -> 2% of each run, Pallas kernels for 0% -> 0%
where the time goes in v1:
time: 243 us; the launch traced here: 241 us
  waiting for transfers between devices  125 us (51%)
  local copies, waits for them, and re-layouts  50.9 us (21%)
  starting transfers between devices  22.5 us (9%)
  matrix products  17.5 us (7%)
  blocking collectives  16.3 us (7%)
  other arithmetic  9.02 us (4%)
    all_to_all x1, waiting for transfers between devices, per_device(): lax.all_to_all(gathered, 'blk', split_axis=0, concat_axis=0, tiled=True)  94 us
    all_to_all x1, waiting for transfers between devices, per_device(): lax.all_to_all(halves.reshape(n_blk, per_owner * record), 'blk', split_ax...  30.9 us
    all_to_all x1, blocking collectives, per_device(): lax.all_to_all(spectra.reshape(n_bin, half_ch * two_seg), 'grp', split_ax...  16.3 us
    all_to_all x1, starting transfers between devices, per_device(): lax.all_to_all(halves.reshape(n_blk, per_owner * record), 'blk', split_ax...  15 us
    reshape x1, local copies, waits for them, and re-layouts, per_device(): other = other.reshape(n_blk, rounds, per_owner, block_ch, two_seg)  11.2 us
    dot_general x1, matrix products, per_device(): jnp.einsum('fcs,rfjs->rfcj', own, both, preferred_element_type=jnp.float32)  10.8 us
    unnamed x8, local copies, waits for them, and re-layouts  8.29 us
    all_to_all x1, starting transfers between devices, per_device(): lax.all_to_all(gathered, 'blk', split_axis=0, concat_axis=0, tiled=True)  7.52 us
  transfers between devices with their start and end apart: 2, of which 2 were waited for; matrix products, arithmetic and copies ran while one was open for 2% of the time, Pallas kernels for 0%

profile of v1, /device:TPU:32, one launch (start us, length us, event | category | flops | bytes accessed | tf_op | source)
XLA Modules:
  0.0 241.4 jit_solution(7694532327071893447)
XLA Ops:
  0.2 0.3 fusion.21
  0.6 1.2 subtract_convert_fusion
  1.7 6.7 %fusion.13 = f32[1024,512]{0,1:T(8,128)} fusion(bf16[1024,2400]{1,0:T(8,128)(2,1)} %bitcast.46, bf16[2400,256]{1,0:T(8,128)(2,1)S(1)} %bitcast.44, bf16[2400,256]{1,0:T(8,128)(2,1)S(1)} %bitcast.43), kind=kOutput, calls=%fused_computation.17 | convolution fusion | flops 2521497600 | bytes 9469952 | tf_op jit(solution)/shard_map/dot_general | solution.py:34
  8.4 1.9 copy.21
  10.9 0.6 copy.22
  11.9 16.3 %all_to_all.33 = bf16[2,128,2048]{1,2,0:T(8,128)(2,1)S(1)} all-to-all(bf16[2,128,2048]{1,2,0:T(8,128)(2,1)S(1)} %copy.23), channel_id=1, replica_groups=mesh['blk'=128,'grp'=2] {'grp'}, dimensions={0} | all-to-all | bytes 2097152 | tf_op jit(solution)/shard_map/all_to_all | solution.py:53
  28.3 0.5 broadcast.152
  28.8 1.4 reduce
  30.2 0.5 copy.38
  30.8 1.6 reshape.159
  32.4 15.0 %all-to-all-start.1 = ((bf16[128,2,2048]{2,1,0:T(2,128)(2,1)}), bf16[128,2,2048]{2,1,0:T(2,128)(2,1)S(1)}, u32[]{:S(2)}, u32[]{:S(2)}) async-start(bf16[128,2,2048]{2,1,0:T(2,128)(2,1)} %reshape.159), calls=%async_computation.1 | async-start | bytes 2097152 | tf_op jit(solution)/shard_map/all_to_all | solution.py:58
  47.4 30.9 %all-to-all-done.1 = bf16[128,2,2048]{2,1,0:T(2,128)(2,1)S(1)} async-done(((bf16[128,2,2048]{2,1,0:T(2,128)(2,1)}), bf16[128,2,2048]{2,1,0:T(2,128)(2,1)S(1)}, u32[]{:S(2)}, u32[]{:S(2)}) %all-to-all-start.1) | async-done | bytes 1048608 | tf_op jit(solution)/shard_map/all_to_all | solution.py:58
  78.3 3.4 %reshape.160 = bf16[128,1,4096]{2,1,0:T(2,128)(2,1)} reshape(bf16[128,2,2048]{2,1,0:T(2,128)(2,1)S(1)} %all-to-all-done.1) | data formatting | bytes 2097152
  81.7 2.7 %copy.37 = bf16[128,1,4096]{2,0,1:T(8,128)(2,1)S(1)} copy(bf16[128,1,4096]{2,1,0:T(2,128)(2,1)} %reshape.160) | data formatting | bytes 2097152
  84.5 4.0 %gather_fusion = bf16[384,4096]{1,0:T(8,128)(2,1)} fusion(bf16[128,4096]{1,0:T(8,128)(2,1)S(1)} %bitcast.33, s32[1024]{0:T(1024)S(1)} %pad_clamp_fusion), kind=kCustom, calls=%fused_computation | custom fusion | bytes 6292992 | tf_op jit(solution)/shard_map/jit(_take)/gather | solution.py:62
  88.5 6.6 %copy.36 = bf16[3,128,4096]{2,0,1:T(4,128)(2,1)} copy(bf16[3,128,4096]{2,1,0:T(8,128)(2,1)} %bitcast.39) | data formatting | bytes 6291456 | tf_op jit(solution)/shard_map/reshape | solution.py:63
  95.1 7.5 %all-to-all-start.2 = ((bf16[128,3,4096]{2,1,0:T(4,128)(2,1)}), bf16[128,3,4096]{2,1,0:T(4,128)(2,1)}, u32[]{:S(2)}, u32[]{:S(2)}) async-start(bf16[128,3,4096]{2,1,0:T(4,128)(2,1)} %bitcast.38), calls=%async_computation.2 | async-start | bytes 8388608 | tf_op jit(solution)/shard_map/all_to_all | solution.py:64
  102.7 3.8 %copy.30 = bf16[128,64,64,1]{2,1,3,0:T(8,128)(2,1)} copy(bf16[128,64,64,1]{0,2,1,3:T(8,128)(2,1)S(1)} %bitcast.42) | data formatting | bytes 2097152 | tf_op jit(solution)/shard_map/reshape | solution.py:69
  106.4 94.0 %all-to-all-done.2 = bf16[128,3,4096]{2,1,0:T(4,128)(2,1)} async-done(((bf16[128,3,4096]{2,1,0:T(4,128)(2,1)}), bf16[128,3,4096]{2,1,0:T(4,128)(2,1)}, u32[]{:S(2)}, u32[]{:S(2)}) %all-to-all-start.2) | async-done | bytes 3145760 | tf_op jit(solution)/shard_map/all_to_all | solution.py:64
  200.4 6.1 %copy.26 = bf16[128,3,4096]{0,2,1:T(8,128)(2,1)S(1)} copy(bf16[128,3,4096]{2,1,0:T(4,128)(2,1)} %all-to-all-done.2) | data formatting | bytes 6291456 | tf_op jit(solution)/shard_map/all_to_all | solution.py:64
  206.5 11.2 %copy.27 = bf16[128,3,1,64,64]{3,4,1,0,2:T(8,128)(2,1)} copy(bf16[128,3,1,64,64]{0,4,3,1,2:T(8,128)(2,1)S(1)} %bitcast.40) | data formatting | bytes 6291456 | tf_op jit(solution)/shard_map/reshape | solution.py:66
  217.8 5.3 %slice_negate_fusion = (bf16[3,128,64,32]{2,3,0,1:T(8,128)(2,1)S(1)}, bf16[3,128,64,32]{2,3,0,1:T(8,128)(2,1)}) fusion(bf16[3,128,64,64]{2,3,0,1:T(8,128)(2,1)} %bitcast.34), kind=kLoop, calls=%fused_computation.10 | loop fusion | flops 786432 | bytes 6291456 | tf_op jit(solution)/shard_map/neg | solution.py:70
  223.1 10.8 %fusion = bf16[3,128,64,128]{3,2,0,1:T(8,128)(2,1)} fusion(bf16[128,64,64,1]{2,1,3,0:T(8,128)(2,1)} %copy.30, bf16[3,128,64,32]{2,3,0,1:T(8,128)(2,1)} %get-tuple-element.6, bf16[3,128,64,32]{2,3,0,1:T(8,128)(2,1)S(1)} %get-tuple-element.5, bf16[3,128,64,64]{2,3,0,1:T(8,128)(2,1)S(1)} %bitcast.35), kind=kOutput, calls=%fused_computation.2 | convolution fusion | flops 427819008 | bytes 13631488 | tf_op jit(solution)/shard_map/fcs,rfjs->rfcj/dot_general | solution.py:72
  233.9 7.5 %copy.29 = bf16[3,128,64,128]{3,2,1,0:T(8,128)(2,1)} copy(bf16[3,128,64,128]{3,2,0,1:T(8,128)(2,1)} %fusion) | data formatting | bytes 12582912 | tf_op jit(solution)/shard_map/convert_element_type | solution.py:73
  (14 shorter events, 1.2 us)
Async XLA Ops:
  30.2 17.1 %copy-start.1 = (s32[3,128]{1,0:T(4,128)S(1)}, s32[3,128]{1,0:T(4,128)}, u32[]{:S(2)}) copy-start(s32[3,128]{1,0:T(4,128)} %param.3) | copy-start | bytes 4612
  32.4 46.0 %all-to-all-start.1 = ((bf16[128,2,2048]{2,1,0:T(2,128)(2,1)}), bf16[128,2,2048]{2,1,0:T(2,128)(2,1)S(1)}, u32[]{:S(2)}, u32[]{:S(2)}) async-start(bf16[128,2,2048]{2,1,0:T(2,128)(2,1)} %reshape.159), calls=%async_computation.1 | async-start | bytes 2097152 | tf_op jit(solution)/shard_map/all_to_all | solution.py:58
  95.1 105.3 %all-to-all-start.2 = ((bf16[128,3,4096]{2,1,0:T(4,128)(2,1)}), bf16[128,3,4096]{2,1,0:T(4,128)(2,1)}, u32[]{:S(2)}, u32[]{:S(2)}) async-start(bf16[128,3,4096]{2,1,0:T(4,128)(2,1)} %bitcast.38), calls=%async_computation.2 | async-start | bytes 8388608 | tf_op jit(solution)/shard_map/all_to_all | solution.py:64
  217.8 5.3 %copy-start = (bf16[128,3,1,64,64]{3,4,1,0,2:T(8,128)(2,1)S(1)}, bf16[128,3,1,64,64]{3,4,1,0,2:T(8,128)(2,1)}, u32[]{:S(2)}) copy-start(bf16[128,3,1,64,64]{3,4,1,0,2:T(8,128)(2,1)} %copy.27) | copy-start | bytes 9437188

commit v2 on v1

--- a/solution.py
+++ b/solution.py
@@ -3,9 +3,12 @@
 import jax
 import jax.numpy as jnp
 from jax import lax
+from jax.experimental import pallas as pl
+from jax.experimental.pallas import tpu as pltpu
 from jax.sharding import PartitionSpec as P
 
 F = 256
+INTERPRET = False
 
 
 first_bin = 8
@@ -40,37 +43,71 @@
     imag_part = spectrum[:, :, num_bins:]
     bin_power = jnp.mean(real_part * real_part + imag_part * imag_part, axis=0)
     factor = lax.rsqrt(bin_power + epsilon)
-    joined = jnp.concatenate([real_part * factor, imag_part * factor], axis=0)
-    return jnp.transpose(joined, (2, 1, 0)).astype(jnp.bfloat16)
+    joined = jnp.stack([real_part * factor, imag_part * factor], axis=1)
+    return jnp.transpose(joined, (3, 0, 1, 2)).astype(jnp.bfloat16)
+
+
+def cross_kernel(scale, ar_ref, ai_ref, rec_ref, out_ref):
+    bins, rounds = rec_ref.shape[0], rec_ref.shape[1]
+    width = out_ref.shape[-1]
+    lane = lax.broadcasted_iota(jnp.int32, out_ref.shape[2:], 1)
+    sign = jnp.where(lane < width // 2, scale, -scale).astype(jnp.float32)
+    for f in range(bins):
+        ar = ar_ref[f]
+        ai = ai_ref[f]
+        for r in range(rounds):
+            rec = rec_ref[f, r]
+            p1 = jnp.dot(ar, rec, preferred_element_type=jnp.float32)
+            p2 = jnp.dot(ai, rec, preferred_element_type=jnp.float32)
+            out = pltpu.roll(p2, width // 2, 1) * scale + p1 * sign
+            out_ref[r, f] = out.astype(out_ref.dtype)
+
+
+def cross(ar, ai, rec, scale):
+    own_bins, block_ch, seg_count = ar.shape
+    rounds, width = rec.shape[1], rec.shape[-1]
+    fb = 8
+    return pl.pallas_call(
+        lambda *refs: cross_kernel(scale, *refs),
+        grid=(own_bins // fb,),
+        in_specs=[
+            pl.BlockSpec((fb, block_ch, seg_count), lambda i: (i, 0, 0)),
+            pl.BlockSpec((fb, block_ch, seg_count), lambda i: (i, 0, 0)),
+            pl.BlockSpec((fb, rounds, seg_count, width), lambda i: (i, 0, 0, 0)),
+        ],
+        out_specs=pl.BlockSpec((rounds, fb, block_ch, width), lambda i: (0, i, 0, 0)),
+        out_shape=jax.ShapeDtypeStruct((rounds, own_bins, block_ch, width), jnp.bfloat16),
+        interpret=INTERPRET,
+    )(ar, ai, rec)
 
 
 def per_device(raw, partner):
     n_blk = lax.axis_size("blk")
+    n_grp = lax.axis_size("grp")
     spectra = whiten(raw, F)
-    n_bin, half_ch, two_seg = spectra.shape
-    seg_count = two_seg // 2
+    n_bin, seg_count, two, half_ch = spectra.shape
     norm_scale = 1.0 / math.sqrt(seg_count)
     halves = lax.all_to_all(
-        spectra.reshape(n_bin, half_ch * two_seg), "grp", split_axis=0, concat_axis=1, tiled=True
+        spectra[:, :, :, None], "grp", split_axis=0, concat_axis=3, tiled=True
     )
-    own_bins, record = halves.shape
+    own_bins = halves.shape[0]
+    block_ch = n_grp * half_ch
+    halves = halves.reshape(own_bins, seg_count, two, block_ch)
+    width = two * block_ch
     per_owner = own_bins // n_blk
     owned = lax.all_to_all(
-        halves.reshape(n_blk, per_owner * record), "blk", split_axis=0, concat_axis=0, tiled=True
+        halves.reshape(n_blk, per_owner * seg_count, width), "blk", split_axis=0, concat_axis=0, tiled=True
     )
     rounds = partner.shape[0]
-    gathered = jnp.take(owned, partner.reshape(-1), axis=0, mode="clip")
-    gathered = jnp.transpose(gathered.reshape(rounds, n_blk, per_owner * record), (1, 0, 2))
+    gathered = jnp.take(owned, jnp.transpose(partner).reshape(-1), axis=0, mode="clip")
+    gathered = gathered.reshape(n_blk, rounds, per_owner, seg_count, width)
+    gathered = jnp.transpose(gathered, (0, 2, 1, 3, 4)).reshape(n_blk, per_owner * rounds * seg_count, width)
     other = lax.all_to_all(gathered, "blk", split_axis=0, concat_axis=0, tiled=True)
-    block_ch = record // two_seg
-    other = other.reshape(n_blk, rounds, per_owner, block_ch, two_seg)
-    other = jnp.transpose(other, (1, 0, 2, 3, 4)).reshape(rounds, own_bins, block_ch, two_seg)
+    other = other.reshape(own_bins, rounds, seg_count, width)
 
-    own = halves.reshape(own_bins, block_ch, two_seg)
-    turned = jnp.concatenate([-other[..., seg_count:], other[..., :seg_count]], axis=-1)
-    both = jnp.concatenate([other, turned], axis=2)
-    result = jnp.einsum("fcs,rfjs->rfcj", own, both, preferred_element_type=jnp.float32)
-    return (result * norm_scale).astype(jnp.bfloat16)
+    ar = jnp.transpose(halves[:, :, 0, :], (0, 2, 1))
+    ai = jnp.transpose(halves[:, :, 1, :], (0, 2, 1))
+    return cross(ar, ai, other, norm_scale)
 
 
 def solution(mesh):

time: 243 us -> 200 us (0.82)
  waiting for transfers between devices: 125 us -> 93.5 us
  Pallas kernels: 0 us -> 14.3 us
  matrix products: 17.5 us -> 6.69 us
  local copies, waits for them, and re-layouts: 50.9 us -> 43.5 us
  other arithmetic: 9.02 us -> 2.25 us
    all_to_all x1, waiting for transfers between devices: 94 us -> 62.9 us  [per_device(): lax.all_to_all(gathered, 'blk', split_axis=0, concat_axis=0, tiled=True)]
    reshape x3 -> x0, local copies, waits for them, and re-layouts: 21.6 us -> none  [the longest x1 11.2 us: per_device(): other = other.reshape(n_blk, rounds, per_owner, block_ch, two_seg)]
    pallas_call x0 -> x1, Pallas kernels: none -> 14.3 us  [cross(): pl.pallas_call(lambda *refs: cross_kernel(scale, *refs), grid=(own_bins /...]
    dot_general x1 -> x0, matrix products: 10.8 us -> none  [per_device(): jnp.einsum('fcs,rfjs->rfcj', own, both, preferred_element_type=jnp.float32)]
    convert_element_type x2 -> x0, local copies, waits for them, and re-layouts: 8.05 us -> none  [the longest x1 7.46 us: per_device(): return (result * norm_scale).astype(jnp.bfloat16)]
    all_to_all x4 -> x3, local copies, waits for them, and re-layouts: 7.01 us -> 14.2 us  [per_device(): lax.all_to_all(spectra[:, :, :, None], 'grp', split_axis=0, concat_axis=3...]
    broadcast_in_dim x0 -> x2, local copies, waits for them, and re-layouts: none -> 6.65 us  [the longest x1 6.45 us: per_device(): spectra[:, :, :, None]]
    neg x1 -> x0, other arithmetic: 5.33 us -> none  [per_device(): -other[..., seg_count:]]
  transfers between devices with their start and end apart: 2 -> 2, of which waited for: 2 -> 2; matrix products, arithmetic and copies ran while one was open for 2% -> 7% of each run, Pallas kernels for 0% -> 0%
where the time goes in v2:
time: 200 us; the launch traced here: 199 us
  waiting for transfers between devices  93.5 us (47%)
  local copies, waits for them, and re-layouts  43.5 us (22%)
  starting transfers between devices  22 us (11%)
  blocking collectives  16.3 us (8%)
  Pallas kernels  14.3 us (7%)
  matrix products  6.69 us (3%)
  other arithmetic  2.25 us (1%)
    all_to_all x1, waiting for transfers between devices, per_device(): lax.all_to_all(gathered, 'blk', split_axis=0, concat_axis=0, tiled=True)  62.9 us
    all_to_all x1, waiting for transfers between devices, per_device(): lax.all_to_all(halves.reshape(n_blk, per_owner * seg_count, width), 'blk'...  30.6 us
    all_to_all x1, blocking collectives, per_device(): lax.all_to_all(spectra[:, :, :, None], 'grp', split_axis=0, concat_axis=3...  16.3 us
    all_to_all x1, starting transfers between devices, per_device(): lax.all_to_all(halves.reshape(n_blk, per_owner * seg_count, width), 'blk'...  15 us
    pallas_call x1, Pallas kernels, cross(): pl.pallas_call(lambda *refs: cross_kernel(scale, *refs), grid=(own_bins /...  14.3 us
    all_to_all x3, local copies, waits for them, and re-layouts, per_device(): lax.all_to_all(spectra[:, :, :, None], 'grp', split_axis=0, concat_axis=3...  14.2 us
    unnamed x8, local copies, waits for them, and re-layouts  10.6 us
    all_to_all x1, starting transfers between devices, per_device(): lax.all_to_all(gathered, 'blk', split_axis=0, concat_axis=0, tiled=True)  7.04 us
  transfers between devices with their start and end apart: 2, of which 2 were waited for; matrix products, arithmetic and copies ran while one was open for 7% of the time, Pallas kernels for 0%

profile of v2, /device:TPU:32, one launch (start us, length us, event | category | flops | bytes accessed | tf_op | source)
XLA Modules:
  0.0 198.8 jit_solution(17437333288869389552)
XLA Ops:
  0.0 0.2 fusion.21
  0.2 0.3 fusion.14
  0.6 1.2 subtract_convert_fusion
  1.7 6.7 %fusion.4 = f32[1024,512]{0,1:T(8,128)} fusion(bf16[1024,2400]{1,0:T(8,128)(2,1)} %bitcast.45, bf16[2400,256]{1,0:T(8,128)(2,1)S(1)} %bitcast.43, bf16[2400,256]{1,0:T(8,128)(2,1)S(1)} %bitcast.42), kind=kOutput, calls=%fused_computation.9 | convolution fusion | flops 2521497600 | bytes 9469952 | tf_op jit(solution)/shard_map/dot_general | solution.py:37
  8.4 1.9 copy.14
  10.3 0.1 add_reduce_fusion
  10.5 0.3 fusion.7
  10.9 6.4 %copy.15 = bf16[256,32,2,1,32]{4,1,2,3,0:T(8,128)(2,1)} copy(bf16[256,32,2,1,32]{0,4,1,2,3:T(8,128)(2,1)S(1)} %maximum_bitcast_fusion) | data formatting | bytes 2097152 | tf_op jit(solution)/shard_map/broadcast_in_dim | solution.py:91
  17.4 5.7 %reshape.143 = bf16[2,2,131072]{2,1,0:T(2,128)(2,1)S(1)} reshape(bf16[256,1,2,32,32]{4,3,2,1,0:T(8,128)(2,1)} %bitcast.34) | data formatting | bytes 2097152
  23.0 16.3 %all_to_all.25 = bf16[2,2,131072]{2,1,0:T(2,128)(2,1)S(1)} all-to-all(bf16[2,2,131072]{2,1,0:T(2,128)(2,1)S(1)} %reshape.143), channel_id=1, replica_groups=mesh['blk'=128,'grp'=2] {'grp'}, dimensions={0} | all-to-all | bytes 2097152 | tf_op jit(solution)/shard_map/all_to_all | solution.py:90
  39.4 3.3 %reshape.144 = bf16[256,1,2,32,32]{4,3,2,1,0:T(8,128)(2,1)} reshape(bf16[2,2,131072]{2,1,0:T(2,128)(2,1)S(1)} %all_to_all.25) | data formatting | bytes 2097152
  42.6 6.3 %copy.21 = bf16[2,128,32,2,1,32]{1,0,5,3,2,4:T(2,128)(2,1)S(1)} copy(bf16[2,128,32,2,1,32]{5,2,3,1,0,4:T(8,128)(2,1)} %bitcast.35) | data formatting | bytes 2097152 | tf_op jit(solution)/shard_map/all_to_all | solution.py:90
  49.0 0.3 copy.18
  49.3 1.7 copy.19
  50.9 15.0 %all-to-all-start.1 = ((bf16[128,32,128]{2,1,0:T(8,128)(2,1)}), bf16[128,32,128]{2,1,0:T(8,128)(2,1)S(1)}, u32[]{:S(2)}, u32[]{:S(2)}) async-start(bf16[128,32,128]{2,1,0:T(8,128)(2,1)} %copy.19), calls=%async_computation.1 | async-start | bytes 2097152 | tf_op jit(solution)/shard_map/all_to_all | solution.py:98
  66.1 0.2 reshape.136
  66.3 30.6 %all-to-all-done.1 = bf16[128,32,128]{2,1,0:T(8,128)(2,1)S(1)} async-done(((bf16[128,32,128]{2,1,0:T(8,128)(2,1)}), bf16[128,32,128]{2,1,0:T(8,128)(2,1)S(1)}, u32[]{:S(2)}, u32[]{:S(2)}) %all-to-all-start.1) | async-done | bytes 1048608 | tf_op jit(solution)/shard_map/all_to_all | solution.py:98
  96.9 3.1 %gather_fusion = bf16[384,32,128]{2,1,0:T(8,128)(2,1)} fusion(bf16[128,32,128]{2,1,0:T(8,128)(2,1)S(1)} %all-to-all-done.1, s32[1024]{0:T(1024)S(1)} %pad_clamp_fusion), kind=kCustom, calls=%fused_computation | custom fusion | bytes 6292992 | tf_op jit(solution)/shard_map/jit(_take)/gather | solution.py:102
  100.0 7.0 %all-to-all-start.2 = ((bf16[128,96,128]{2,1,0:T(8,128)(2,1)}), bf16[128,96,128]{2,1,0:T(8,128)(2,1)S(1)}, u32[]{:S(2)}, u32[]{:S(2)}) async-start(bf16[128,96,128]{2,1,0:T(8,128)(2,1)} %bitcast.37), calls=%async_computation.2 | async-start | bytes 6291456 | tf_op jit(solution)/shard_map/all_to_all | solution.py:105
  107.1 7.6 %copy.17 = bf16[128,32,2,2,1,32]{1,5,3,0,2,4:T(8,128)(2,1)} copy(bf16[128,32,2,2,1,32]{0,3,5,2,1,4:T(2,128)(2,1)} %bitcast.40) | data formatting | bytes 2097152 | tf_op jit(solution)/shard_map/all_to_all | solution.py:90
  114.7 5.2 %slice_bitcast_fusion = (bf16[128,64,32]{2,1,0:T(8,128)(2,1)}, bf16[128,64,32]{2,1,0:T(8,128)(2,1)}) fusion(bf16[128,32,2,64]{1,3,0,2:T(8,128)(2,1)} %bitcast.36), kind=kLoop, calls=%fused_computation.7 | loop fusion | bytes 2097152 | tf_op jit(solution)/shard_map/transpose | solution.py:109
  119.9 62.9 %all-to-all-done.2 = bf16[128,96,128]{2,1,0:T(8,128)(2,1)S(1)} async-done(((bf16[128,96,128]{2,1,0:T(8,128)(2,1)}), bf16[128,96,128]{2,1,0:T(8,128)(2,1)S(1)}, u32[]{:S(2)}, u32[]{:S(2)}) %all-to-all-start.2) | async-done | bytes 3145760 | tf_op jit(solution)/shard_map/all_to_all | solution.py:105
  182.8 1.6 copy-done
  184.4 14.3 %shard_map.28 = bf16[3,128,64,128]{3,2,1,0:T(8,128)(2,1)} custom-call(bf16[128,64,32]{2,1,0:T(8,128)(2,1)} %get-tuple-element.6.refs_0_, bf16[128,64,32]{2,1,0:T(8,128)(2,1)} %get-tuple-element.5.refs_1_, bf16[128,3,32,128]{3,2,1,0:T(8,128)(2,1)} %bitcast.38), custom_call_target="tpu_custom_call" | custom-call | tf_op jit(solution)/shard_map/pallas_call | solution.py:70
  (11 shorter events, 0.3 us)
Async XLA Ops:
  49.0 2.0 copy-start.1
  49.2 16.7 %copy-start.2 = (s32[3,128]{1,0:T(4,128)S(1)}, s32[3,128]{1,0:T(4,128)}, u32[]{:S(2)}) copy-start(s32[3,128]{1,0:T(4,128)} %param.3) | copy-start | bytes 4612
  50.9 45.9 %all-to-all-start.1 = ((bf16[128,32,128]{2,1,0:T(8,128)(2,1)}), bf16[128,32,128]{2,1,0:T(8,128)(2,1)S(1)}, u32[]{:S(2)}, u32[]{:S(2)}) async-start(bf16[128,32,128]{2,1,0:T(8,128)(2,1)} %copy.19), calls=%async_computation.1 | async-start | bytes 2097152 | tf_op jit(solution)/shard_map/all_to_all | solution.py:98
  100.0 82.8 %all-to-all-start.2 = ((bf16[128,96,128]{2,1,0:T(8,128)(2,1)}), bf16[128,96,128]{2,1,0:T(8,128)(2,1)S(1)}, u32[]{:S(2)}, u32[]{:S(2)}) async-start(bf16[128,96,128]{2,1,0:T(8,128)(2,1)} %bitcast.37), calls=%async_computation.2 | async-start | bytes 6291456 | tf_op jit(solution)/shard_map/all_to_all | solution.py:105
  182.8 1.6 copy-start

commit v3 on v2

--- a/solution.py
+++ b/solution.py
@@ -43,8 +43,8 @@
     imag_part = spectrum[:, :, num_bins:]
     bin_power = jnp.mean(real_part * real_part + imag_part * imag_part, axis=0)
     factor = lax.rsqrt(bin_power + epsilon)
-    joined = jnp.stack([real_part * factor, imag_part * factor], axis=1)
-    return jnp.transpose(joined, (3, 0, 1, 2)).astype(jnp.bfloat16)
+    joined = jnp.stack([real_part * factor, imag_part * factor], axis=0)
+    return jnp.transpose(joined, (3, 2, 0, 1)).astype(jnp.bfloat16)
 
 
 def cross_kernel(scale, ar_ref, ai_ref, rec_ref, out_ref):
@@ -85,14 +85,17 @@
     n_blk = lax.axis_size("blk")
     n_grp = lax.axis_size("grp")
     spectra = whiten(raw, F)
-    n_bin, seg_count, two, half_ch = spectra.shape
+    n_bin, half_ch, two, seg_count = spectra.shape
     norm_scale = 1.0 / math.sqrt(seg_count)
     halves = lax.all_to_all(
-        spectra[:, :, :, None], "grp", split_axis=0, concat_axis=3, tiled=True
+        spectra.reshape(n_bin, half_ch * two * seg_count), "grp", split_axis=0, concat_axis=1, tiled=True
     )
     own_bins = halves.shape[0]
     block_ch = n_grp * half_ch
-    halves = halves.reshape(own_bins, seg_count, two, block_ch)
+    halves = halves.reshape(own_bins, block_ch, two, seg_count)
+    ar = halves[:, :, 0, :]
+    ai = halves[:, :, 1, :]
+    halves = jnp.transpose(halves, (0, 3, 2, 1))
     width = two * block_ch
     per_owner = own_bins // n_blk
     owned = lax.all_to_all(
@@ -105,8 +108,6 @@
     other = lax.all_to_all(gathered, "blk", split_axis=0, concat_axis=0, tiled=True)
     other = other.reshape(own_bins, rounds, seg_count, width)
 
-    ar = jnp.transpose(halves[:, :, 0, :], (0, 2, 1))
-    ai = jnp.transpose(halves[:, :, 1, :], (0, 2, 1))
     return cross(ar, ai, other, norm_scale)
 
 

time: 200 us -> 180 us (0.900)
  local copies, waits for them, and re-layouts: 43.5 us -> 23 us
    all_to_all x3 -> x2, local copies, waits for them, and re-layouts: 14.2 us -> 0.43 us  [per_device(): lax.all_to_all(spectra.reshape(n_bin, half_ch * two * seg_count), 'grp',...]
    broadcast_in_dim x1 -> x0, local copies, waits for them, and re-layouts: 6.45 us -> none  [per_device(): spectra[:, :, :, None]]
    transpose x1, local copies, waits for them, and re-layouts: 5.16 us -> 0.68 us  [per_device(): halves = jnp.transpose(halves, (0, 3, 2, 1))]
    slice x0 -> x1, local copies, waits for them, and re-layouts: none -> 2.3 us  [per_device(): ai = halves[:, :, 1, :]]
where the time goes in v3:
time: 180 us; the launch traced here: 179 us
  waiting for transfers between devices  94.7 us (53%)
  local copies, waits for them, and re-layouts  23 us (13%)
  starting transfers between devices  22 us (12%)
  blocking collectives  16.3 us (9%)
  Pallas kernels  14.3 us (8%)
  matrix products  6.69 us (4%)
  other arithmetic  2.25 us (1%)
    all_to_all x1, waiting for transfers between devices, per_device(): lax.all_to_all(gathered, 'blk', split_axis=0, concat_axis=0, tiled=True)  64.1 us
    all_to_all x1, waiting for transfers between devices, per_device(): lax.all_to_all(halves.reshape(n_blk, per_owner * seg_count, width), 'blk'...  30.6 us
    all_to_all x1, blocking collectives, per_device(): lax.all_to_all(spectra.reshape(n_bin, half_ch * two * seg_count), 'grp',...  16.3 us
    all_to_all x1, starting transfers between devices, per_device(): lax.all_to_all(halves.reshape(n_blk, per_owner * seg_count, width), 'blk'...  15 us
    pallas_call x1, Pallas kernels, cross(): pl.pallas_call(lambda *refs: cross_kernel(scale, *refs), grid=(own_bins /...  14.3 us
    unnamed x8, local copies, waits for them, and re-layouts  11.9 us
    all_to_all x1, starting transfers between devices, per_device(): lax.all_to_all(gathered, 'blk', split_axis=0, concat_axis=0, tiled=True)  7.04 us
    dot_general x1, matrix products, whiten(): jnp.dot(samples.reshape(seg_count * chan_count, length), dft_table(length...  6.69 us
  transfers between devices with their start and end apart: 2, of which 2 were waited for; matrix products, arithmetic and copies ran while one was open for 7% of the time, Pallas kernels for 0%

profile of v3, /device:TPU:32, one launch (start us, length us, event | category | flops | bytes accessed | tf_op | source)
XLA Modules:
  0.0 179.4 jit_solution(10114305249473496120)
XLA Ops:
  0.0 0.2 fusion.21
  0.2 0.3 fusion.14
  0.6 1.2 subtract_convert_fusion
  1.7 6.7 %fusion.4 = f32[1024,512]{0,1:T(8,128)} fusion(bf16[1024,2400]{1,0:T(8,128)(2,1)} %bitcast.40, bf16[2400,256]{1,0:T(8,128)(2,1)S(1)} %bitcast.38, bf16[2400,256]{1,0:T(8,128)(2,1)S(1)} %bitcast.37), kind=kOutput, calls=%fused_computation.7 | convolution fusion | flops 2521497600 | bytes 9469952 | tf_op jit(solution)/shard_map/dot_general | solution.py:37
  8.4 1.9 %copy.18 = f32[1024,512]{1,0:T(8,128)S(1)} copy(f32[1024,512]{0,1:T(8,128)} %fusion.4) | data formatting | bytes 4194304 | tf_op jit(solution)/shard_map/dot_general | solution.py:37
  10.3 0.1 add_reduce_fusion
  10.5 0.3 fusion.7
  10.9 0.6 copy.19
  11.5 0.3 all_to_all.18
  11.9 16.3 %all_to_all.26 = bf16[2,128,2048]{1,2,0:T(8,128)(2,1)S(1)} all-to-all(bf16[2,128,2048]{1,2,0:T(8,128)(2,1)S(1)} %copy.20), channel_id=1, replica_groups=mesh['blk'=128,'grp'=2] {'grp'}, dimensions={0} | all-to-all | bytes 2097152 | tf_op jit(solution)/shard_map/all_to_all | solution.py:90
  28.3 1.0 copy-done.1
  29.2 0.7 copy.23
  29.9 1.7 copy.24
  31.6 15.0 %all-to-all-start.1 = ((bf16[128,32,128]{2,1,0:T(8,128)(2,1)}), bf16[128,32,128]{2,1,0:T(8,128)(2,1)S(1)}, u32[]{:S(2)}, u32[]{:S(2)}) async-start(bf16[128,32,128]{2,1,0:T(8,128)(2,1)} %copy.24), calls=%async_computation.1 | async-start | bytes 2097152 | tf_op jit(solution)/shard_map/all_to_all | solution.py:101
  46.7 0.2 reshape.144
  47.0 30.6 %all-to-all-done.1 = bf16[128,32,128]{2,1,0:T(8,128)(2,1)S(1)} async-done(((bf16[128,32,128]{2,1,0:T(8,128)(2,1)}), bf16[128,32,128]{2,1,0:T(8,128)(2,1)S(1)}, u32[]{:S(2)}, u32[]{:S(2)}) %all-to-all-start.1) | async-done | bytes 1048608 | tf_op jit(solution)/shard_map/all_to_all | solution.py:101
  77.6 3.2 %gather_fusion = bf16[384,32,128]{2,1,0:T(8,128)(2,1)} fusion(bf16[128,32,128]{2,1,0:T(8,128)(2,1)S(1)} %all-to-all-done.1, s32[1024]{0:T(1024)S(1)} %pad_clamp_fusion), kind=kCustom, calls=%fused_computation | custom fusion | bytes 6292992 | tf_op jit(solution)/shard_map/jit(_take)/gather | solution.py:105
  80.7 7.0 %all-to-all-start.2 = ((bf16[128,96,128]{2,1,0:T(8,128)(2,1)}), bf16[128,96,128]{2,1,0:T(8,128)(2,1)S(1)}, u32[]{:S(2)}, u32[]{:S(2)}) async-start(bf16[128,96,128]{2,1,0:T(8,128)(2,1)} %bitcast.30), calls=%async_computation.2 | async-start | bytes 6291456 | tf_op jit(solution)/shard_map/all_to_all | solution.py:108
  87.8 2.3 %fusion.24 = (bf16[128,64,1,32]{0,3,2,1:T(8,128)(2,1)}, bf16[128,64,1,32]{0,3,2,1:T(8,128)(2,1)}) fusion(bf16[128,64,2,32]{0,3,2,1:T(8,128)(2,1)} %bitcast.33), kind=kLoop, calls=%fused_computation.37 | loop fusion | bytes 2097152 | tf_op jit(solution)/shard_map/slice | solution.py:97
  90.1 4.6 %copy.27 = bf16[128,64,1,32]{3,1,0,2:T(8,128)(2,1)} copy(bf16[128,64,1,32]{0,3,2,1:T(8,128)(2,1)} %get-tuple-element.7) | data formatting | bytes 1048576
  94.7 4.7 %copy.26 = bf16[128,64,1,32]{3,1,0,2:T(8,128)(2,1)} copy(bf16[128,64,1,32]{0,3,2,1:T(8,128)(2,1)} %get-tuple-element.8) | data formatting | bytes 1048576
  99.4 64.1 %all-to-all-done.2 = bf16[128,96,128]{2,1,0:T(8,128)(2,1)S(1)} async-done(((bf16[128,96,128]{2,1,0:T(8,128)(2,1)}), bf16[128,96,128]{2,1,0:T(8,128)(2,1)S(1)}, u32[]{:S(2)}, u32[]{:S(2)}) %all-to-all-start.2) | async-done | bytes 3145760 | tf_op jit(solution)/shard_map/all_to_all | solution.py:108
  163.5 1.6 copy-done
  165.1 14.3 %shard_map.28 = bf16[3,128,64,128]{3,2,1,0:T(8,128)(2,1)} custom-call(bf16[128,64,32]{2,1,0:T(8,128)(2,1)} %bitcast.35, bf16[128,64,32]{2,1,0:T(8,128)(2,1)} %bitcast.34, bf16[128,3,32,128]{3,2,1,0:T(8,128)(2,1)} %bitcast.31), custom_call_target="tpu_custom_call" | custom-call | tf_op jit(solution)/shard_map/pallas_call | solution.py:70
  (11 shorter events, 0.4 us)
Async XLA Ops:
  28.3 1.0 copy-start.1
  29.9 16.7 %copy-start.2 = (s32[3,128]{1,0:T(4,128)S(1)}, s32[3,128]{1,0:T(4,128)}, u32[]{:S(2)}) copy-start(s32[3,128]{1,0:T(4,128)} %param.3) | copy-start | bytes 4612
  31.6 45.9 %all-to-all-start.1 = ((bf16[128,32,128]{2,1,0:T(8,128)(2,1)}), bf16[128,32,128]{2,1,0:T(8,128)(2,1)S(1)}, u32[]{:S(2)}, u32[]{:S(2)}) async-start(bf16[128,32,128]{2,1,0:T(8,128)(2,1)} %copy.24), calls=%async_computation.1 | async-start | bytes 2097152 | tf_op jit(solution)/shard_map/all_to_all | solution.py:101
  80.7 82.8 %all-to-all-start.2 = ((bf16[128,96,128]{2,1,0:T(8,128)(2,1)}), bf16[128,96,128]{2,1,0:T(8,128)(2,1)S(1)}, u32[]{:S(2)}, u32[]{:S(2)}) async-start(bf16[128,96,128]{2,1,0:T(8,128)(2,1)} %bitcast.30), calls=%async_computation.2 | async-start | bytes 6291456 | tf_op jit(solution)/shard_map/all_to_all | solution.py:108
  163.5 1.6 copy-start

commit v4 on v3

--- a/solution.py
+++ b/solution.py
@@ -47,38 +47,37 @@
     return jnp.transpose(joined, (3, 2, 0, 1)).astype(jnp.bfloat16)
 
 
-def cross_kernel(scale, ar_ref, ai_ref, rec_ref, out_ref):
+def cross_kernel(scale, a_ref, rec_ref, out_ref):
     bins, rounds = rec_ref.shape[0], rec_ref.shape[1]
-    width = out_ref.shape[-1]
-    lane = lax.broadcasted_iota(jnp.int32, out_ref.shape[2:], 1)
+    block_ch, width = out_ref.shape[2], out_ref.shape[3]
+    lane = lax.broadcasted_iota(jnp.int32, (block_ch, width), 1)
     sign = jnp.where(lane < width // 2, scale, -scale).astype(jnp.float32)
     for f in range(bins):
-        ar = ar_ref[f]
-        ai = ai_ref[f]
+        a = a_ref[f]
         for r in range(rounds):
-            rec = rec_ref[f, r]
-            p1 = jnp.dot(ar, rec, preferred_element_type=jnp.float32)
-            p2 = jnp.dot(ai, rec, preferred_element_type=jnp.float32)
+            both = jnp.dot(a, rec_ref[f, r], preferred_element_type=jnp.float32)
+            p1 = both[:block_ch]
+            p2 = both[block_ch:]
             out = pltpu.roll(p2, width // 2, 1) * scale + p1 * sign
             out_ref[r, f] = out.astype(out_ref.dtype)
 
 
-def cross(ar, ai, rec, scale):
-    own_bins, block_ch, seg_count = ar.shape
+def cross(a, rec, scale):
+    own_bins, two_ch, seg_count = a.shape
     rounds, width = rec.shape[1], rec.shape[-1]
-    fb = 8
+    block_ch = two_ch // 2
+    fb = 16
     return pl.pallas_call(
         lambda *refs: cross_kernel(scale, *refs),
         grid=(own_bins // fb,),
         in_specs=[
-            pl.BlockSpec((fb, block_ch, seg_count), lambda i: (i, 0, 0)),
-            pl.BlockSpec((fb, block_ch, seg_count), lambda i: (i, 0, 0)),
+            pl.BlockSpec((fb, two_ch, seg_count), lambda i: (i, 0, 0)),
             pl.BlockSpec((fb, rounds, seg_count, width), lambda i: (i, 0, 0, 0)),
         ],
         out_specs=pl.BlockSpec((rounds, fb, block_ch, width), lambda i: (0, i, 0, 0)),
         out_shape=jax.ShapeDtypeStruct((rounds, own_bins, block_ch, width), jnp.bfloat16),
         interpret=INTERPRET,
-    )(ar, ai, rec)
+    )(a, rec)
 
 
 def per_device(raw, partner):
@@ -93,8 +92,7 @@
     own_bins = halves.shape[0]
     block_ch = n_grp * half_ch
     halves = halves.reshape(own_bins, block_ch, two, seg_count)
-    ar = halves[:, :, 0, :]
-    ai = halves[:, :, 1, :]
+    own = jnp.transpose(halves, (0, 2, 1, 3)).reshape(own_bins, two * block_ch, seg_count)
     halves = jnp.transpose(halves, (0, 3, 2, 1))
     width = two * block_ch
     per_owner = own_bins // n_blk
@@ -108,7 +106,7 @@
     other = lax.all_to_all(gathered, "blk", split_axis=0, concat_axis=0, tiled=True)
     other = other.reshape(own_bins, rounds, seg_count, width)
 
-    return cross(ar, ai, other, norm_scale)
+    return cross(own, other, norm_scale)
 
 
 def solution(mesh):

time: 180 us -> 175 us (0.972)
  Pallas kernels: 14.3 us -> 9.71 us
  local copies, waits for them, and re-layouts: 23 us -> 18.7 us
  waiting for transfers between devices: 94.7 us -> 99 us
    unnamed x8 -> x6, local copies, waits for them, and re-layouts: 11.9 us -> 2.64 us
    transpose x0 -> x1, local copies, waits for them, and re-layouts: none -> 7.31 us  [per_device(): jnp.transpose(halves, (0, 2, 1, 3))]
    pallas_call x1, Pallas kernels: 14.3 us -> 9.71 us  [cross(): pl.pallas_call(lambda *refs: cross_kernel(scale, *refs), grid=(own_bins /...]
    all_to_all x1, waiting for transfers between devices: 64.1 us -> 68.4 us  [per_device(): lax.all_to_all(gathered, 'blk', split_axis=0, concat_axis=0, tiled=True)]
    slice x1 -> x0, local copies, waits for them, and re-layouts: 2.3 us -> none  [per_device(): ai = halves[:, :, 1, :]]
  transfers between devices with their start and end apart: 2 -> 2, of which waited for: 2 -> 2; matrix products, arithmetic and copies ran while one was open for 7% -> 4% of each run, Pallas kernels for 0% -> 0%
where the time goes in v4:
time: 175 us
  waiting for transfers between devices  99 us (57%)
  starting transfers between devices  22 us (13%)
  local copies, waits for them, and re-layouts  18.7 us (11%)
  blocking collectives  16.3 us (9%)
  Pallas kernels  9.71 us (6%)
  matrix products  6.69 us (4%)
  other arithmetic  2.25 us (1%)
    all_to_all x1, waiting for transfers between devices, per_device(): lax.all_to_all(gathered, 'blk', split_axis=0, concat_axis=0, tiled=True)  68.4 us
    all_to_all x1, waiting for transfers between devices, per_device(): lax.all_to_all(halves.reshape(n_blk, per_owner * seg_count, width), 'blk'...  30.6 us
    all_to_all x1, blocking collectives, per_device(): lax.all_to_all(spectra.reshape(n_bin, half_ch * two * seg_count), 'grp',...  16.3 us
    all_to_all x1, starting transfers between devices, per_device(): lax.all_to_all(halves.reshape(n_blk, per_owner * seg_count, width), 'blk'...  15 us
    pallas_call x1, Pallas kernels, cross(): pl.pallas_call(lambda *refs: cross_kernel(scale, *refs), grid=(own_bins /...  9.71 us
    transpose x1, local copies, waits for them, and re-layouts, per_device(): jnp.transpose(halves, (0, 2, 1, 3))  7.31 us
    all_to_all x1, starting transfers between devices, per_device(): lax.all_to_all(gathered, 'blk', split_axis=0, concat_axis=0, tiled=True)  7.04 us
    dot_general x1, matrix products, whiten(): jnp.dot(samples.reshape(seg_count * chan_count, length), dft_table(length...  6.69 us
  transfers between devices with their start and end apart: 2, of which 2 were waited for; matrix products, arithmetic and copies ran while one was open for 4% of the time, Pallas kernels for 0%

profile of v4, /device:TPU:32, one launch (start us, length us, event | category | flops | bytes accessed | tf_op | source)
XLA Modules:
  0.0 174.9 jit_solution(7169937349577978281)
XLA Ops:
  0.0 0.2 fusion.21
  0.2 0.3 fusion.14
  0.6 1.2 subtract_convert_fusion
  1.7 6.7 %fusion.4 = f32[1024,512]{0,1:T(8,128)} fusion(bf16[1024,2400]{1,0:T(8,128)(2,1)} %bitcast.40, bf16[2400,256]{1,0:T(8,128)(2,1)S(1)} %bitcast.38, bf16[2400,256]{1,0:T(8,128)(2,1)S(1)} %bitcast.37), kind=kOutput, calls=%fused_computation.7 | convolution fusion | flops 2521497600 | bytes 9469952 | tf_op jit(solution)/shard_map/dot_general | solution.py:37
  8.4 1.9 %copy.16 = f32[1024,512]{1,0:T(8,128)S(1)} copy(f32[1024,512]{0,1:T(8,128)} %fusion.4) | data formatting | bytes 4194304 | tf_op jit(solution)/shard_map/dot_general | solution.py:37
  10.3 0.1 add_reduce_fusion
  10.5 0.3 fusion.7
  10.9 0.6 copy.17
  11.5 0.3 all_to_all.18
  11.8 0.1 copy.18
  11.9 16.3 %all_to_all.26 = bf16[2,128,2048]{1,2,0:T(8,128)(2,1)S(1)} all-to-all(bf16[2,128,2048]{1,2,0:T(8,128)(2,1)S(1)} %copy.18), channel_id=1, replica_groups=mesh['blk'=128,'grp'=2] {'grp'}, dimensions={0} | all-to-all | bytes 2097152 | tf_op jit(solution)/shard_map/all_to_all | solution.py:89
  28.3 1.0 copy-done.1
  29.2 0.7 copy.20
  29.9 1.7 copy.21
  31.6 15.0 %all-to-all-start.1 = ((bf16[128,32,128]{2,1,0:T(8,128)(2,1)}), bf16[128,32,128]{2,1,0:T(8,128)(2,1)S(1)}, u32[]{:S(2)}, u32[]{:S(2)}) async-start(bf16[128,32,128]{2,1,0:T(8,128)(2,1)} %copy.21), calls=%async_computation.1 | async-start | bytes 2097152 | tf_op jit(solution)/shard_map/all_to_all | solution.py:99
  46.6 0.1 copy.22
  46.7 0.2 reshape.148
  47.0 30.6 %all-to-all-done.1 = bf16[128,32,128]{2,1,0:T(8,128)(2,1)S(1)} async-done(((bf16[128,32,128]{2,1,0:T(8,128)(2,1)}), bf16[128,32,128]{2,1,0:T(8,128)(2,1)S(1)}, u32[]{:S(2)}, u32[]{:S(2)}) %all-to-all-start.1) | async-done | bytes 1048608 | tf_op jit(solution)/shard_map/all_to_all | solution.py:99
  77.6 3.2 %gather_fusion = bf16[384,32,128]{2,1,0:T(8,128)(2,1)} fusion(bf16[128,32,128]{2,1,0:T(8,128)(2,1)S(1)} %all-to-all-done.1, s32[1024]{0:T(1024)S(1)} %pad_clamp_fusion), kind=kCustom, calls=%fused_computation | custom fusion | bytes 6292992 | tf_op jit(solution)/shard_map/jit(_take)/gather | solution.py:103
  80.7 7.0 %all-to-all-start.2 = ((bf16[128,96,128]{2,1,0:T(8,128)(2,1)}), bf16[128,96,128]{2,1,0:T(8,128)(2,1)S(1)}, u32[]{:S(2)}, u32[]{:S(2)}) async-start(bf16[128,96,128]{2,1,0:T(8,128)(2,1)} %bitcast.32), calls=%async_computation.2 | async-start | bytes 6291456 | tf_op jit(solution)/shard_map/all_to_all | solution.py:106
  87.8 7.3 %copy.19 = bf16[128,2,64,32]{3,2,1,0:T(8,128)(2,1)} copy(bf16[128,2,64,32]{0,3,1,2:T(8,128)(2,1)} %bitcast.35) | data formatting | bytes 2097152 | tf_op jit(solution)/shard_map/transpose | solution.py:95
  95.1 68.4 %all-to-all-done.2 = bf16[128,96,128]{2,1,0:T(8,128)(2,1)S(1)} async-done(((bf16[128,96,128]{2,1,0:T(8,128)(2,1)}), bf16[128,96,128]{2,1,0:T(8,128)(2,1)S(1)}, u32[]{:S(2)}, u32[]{:S(2)}) %all-to-all-start.2) | async-done | bytes 3145760 | tf_op jit(solution)/shard_map/all_to_all | solution.py:106
  163.5 1.7 copy-done
  165.1 9.7 %shard_map.28 = bf16[3,128,64,128]{3,2,1,0:T(8,128)(2,1)} custom-call(bf16[128,128,32]{2,1,0:T(8,128)(2,1)} %bitcast.31, bf16[128,3,32,128]{3,2,1,0:T(8,128)(2,1)} %bitcast.33), custom_call_target="tpu_custom_call" | custom-call | tf_op jit(solution)/shard_map/pallas_call | solution.py:70
  (9 shorter events, 0.1 us)
Async XLA Ops:
  28.3 1.0 copy-start.1
  29.9 16.7 %copy-start.2 = (s32[3,128]{1,0:T(4,128)S(1)}, s32[3,128]{1,0:T(4,128)}, u32[]{:S(2)}) copy-start(s32[3,128]{1,0:T(4,128)} %param.3) | copy-start | bytes 4612
  31.6 45.9 %all-to-all-start.1 = ((bf16[128,32,128]{2,1,0:T(8,128)(2,1)}), bf16[128,32,128]{2,1,0:T(8,128)(2,1)S(1)}, u32[]{:S(2)}, u32[]{:S(2)}) async-start(bf16[128,32,128]{2,1,0:T(8,128)(2,1)} %copy.21), calls=%async_computation.1 | async-start | bytes 2097152 | tf_op jit(solution)/shard_map/all_to_all | solution.py:99
  80.7 82.8 %all-to-all-start.2 = ((bf16[128,96,128]{2,1,0:T(8,128)(2,1)}), bf16[128,96,128]{2,1,0:T(8,128)(2,1)S(1)}, u32[]{:S(2)}, u32[]{:S(2)}) async-start(bf16[128,96,128]{2,1,0:T(8,128)(2,1)} %bitcast.32), calls=%async_computation.2 | async-start | bytes 6291456 | tf_op jit(solution)/shard_map/all_to_all | solution.py:106
  163.5 1.7 copy-start

commit v5 on v4

--- a/solution.py
+++ b/solution.py
@@ -93,12 +93,13 @@
     block_ch = n_grp * half_ch
     halves = halves.reshape(own_bins, block_ch, two, seg_count)
     own = jnp.transpose(halves, (0, 2, 1, 3)).reshape(own_bins, two * block_ch, seg_count)
-    halves = jnp.transpose(halves, (0, 3, 2, 1))
     width = two * block_ch
     per_owner = own_bins // n_blk
-    owned = lax.all_to_all(
-        halves.reshape(n_blk, per_owner * seg_count, width), "blk", split_axis=0, concat_axis=0, tiled=True
-    )
+    order = spectra.reshape(n_grp, n_blk, per_owner, half_ch * two * seg_count)
+    order = jnp.transpose(order, (1, 0, 2, 3)).reshape(n_bin, half_ch * two * seg_count)
+    owned = lax.all_to_all(order, ("blk", "grp"), split_axis=0, concat_axis=0, tiled=True)
+    owned = owned.reshape(n_blk, n_grp, per_owner, half_ch, two, seg_count)
+    owned = jnp.transpose(owned, (0, 2, 5, 4, 1, 3)).reshape(n_blk, per_owner * seg_count, width)
     rounds = partner.shape[0]
     gathered = jnp.take(owned, jnp.transpose(partner).reshape(-1), axis=0, mode="clip")
     gathered = gathered.reshape(n_blk, rounds, per_owner, seg_count, width)

time: 175 us -> 213 us (1.22)
  local copies, waits for them, and re-layouts: 18.7 us -> 55.5 us
  blocking collectives: 16.3 us -> 0 us
  other arithmetic: 2.25 us -> 17.1 us
  starting transfers between devices: 22 us -> 25.5 us
    all_to_all x1 -> x0, blocking collectives: 16.3 us -> none  [per_device(): lax.all_to_all(spectra.reshape(n_bin, half_ch * two * seg_count), 'grp',...]
    all_to_all x0 -> x2, other arithmetic: none -> 14.9 us  [per_device(): lax.all_to_all(order, ('blk', 'grp'), split_axis=0, concat_axis=0, tiled=...]
    transpose x1 -> x2, local copies, waits for them, and re-layouts: 0.68 us -> 10.8 us  [the longest x1 7.03 us: per_device(): jnp.transpose(owned, (0, 2, 5, 4, 1, 3))]
    reshape x1 -> x3, local copies, waits for them, and re-layouts: 1.68 us -> 11.1 us  [the longest x1 9.87 us: per_device(): owned = owned.reshape(n_blk, n_grp, per_owner, half_ch, two, seg_count)]
    unnamed x6 -> x10, local copies, waits for them, and re-layouts: 2.64 us -> 11.9 us
    all_to_all x0 -> x2, local copies, waits for them, and re-layouts: none -> 6.99 us  [per_device(): lax.all_to_all(order, ('blk', 'grp'), split_axis=0, concat_axis=0, tiled=...]
    all_to_all x1 -> x2, starting transfers between devices: 15 us -> 18 us  [the longest x1 14.4 us: per_device(): lax.all_to_all(order, ('blk', 'grp'), split_axis=0, concat_axis=0, tiled=...]
    all_to_all x1 -> x2, waiting for transfers between devices: 30.6 us -> 29.2 us  [the longest x1 29.2 us: per_device(): lax.all_to_all(order, ('blk', 'grp'), split_axis=0, concat_axis=0, tiled=...]
  transfers between devices with their start and end apart: 2 -> 3, of which waited for: 2 -> 2; matrix products, arithmetic and copies ran while one was open for 4% -> 21% of each run, Pallas kernels for 0% -> 0%
where the time goes in v5:
time: 213 us; the launch traced here: 212 us
  waiting for transfers between devices  97.6 us (46%)
  local copies, waits for them, and re-layouts  55.5 us (26%)
  starting transfers between devices  25.5 us (12%)
  other arithmetic  17.1 us (8%)
  Pallas kernels  9.69 us (5%)
  matrix products  6.69 us (3%)
    all_to_all x1, waiting for transfers between devices, per_device(): lax.all_to_all(gathered, 'blk', split_axis=0, concat_axis=0, tiled=True)  68.4 us
    all_to_all x1, waiting for transfers between devices, per_device(): lax.all_to_all(order, ('blk', 'grp'), split_axis=0, concat_axis=0, tiled=...  29.2 us
    all_to_all x2, other arithmetic, per_device(): lax.all_to_all(order, ('blk', 'grp'), split_axis=0, concat_axis=0, tiled=...  14.9 us
    all_to_all x1, starting transfers between devices, per_device(): lax.all_to_all(order, ('blk', 'grp'), split_axis=0, concat_axis=0, tiled=...  14.4 us
    unnamed x10, local copies, waits for them, and re-layouts  11.9 us
    reshape x1, local copies, waits for them, and re-layouts, per_device(): owned = owned.reshape(n_blk, n_grp, per_owner, half_ch, two, seg_count)  9.87 us
    pallas_call x1, Pallas kernels, cross(): pl.pallas_call(lambda *refs: cross_kernel(scale, *refs), grid=(own_bins /...  9.69 us
    all_to_all x1, starting transfers between devices, per_device(): lax.all_to_all(gathered, 'blk', split_axis=0, concat_axis=0, tiled=True)  7.5 us
  transfers between devices with their start and end apart: 3, of which 2 were waited for; matrix products, arithmetic and copies ran while one was open for 21% of the time, Pallas kernels for 0%

profile of v5, /device:TPU:32, one launch (start us, length us, event | category | flops | bytes accessed | tf_op | source)
XLA Modules:
  0.0 212.2 jit_solution(5194508150998193391)
XLA Ops:
  0.6 1.2 subtract_convert_fusion
  1.7 6.7 %fusion.4 = f32[1024,512]{0,1:T(8,128)} fusion(bf16[1024,2400]{1,0:T(8,128)(2,1)} %bitcast.47, bf16[2400,256]{1,0:T(8,128)(2,1)S(1)} %bitcast.45, bf16[2400,256]{1,0:T(8,128)(2,1)S(1)} %bitcast.44), kind=kOutput, calls=%fused_computation.7 | convolution fusion | flops 2521497600 | bytes 9469952 | tf_op jit(solution)/shard_map/dot_general | solution.py:37
  8.4 1.9 copy.20
  10.9 0.6 copy.21
  11.8 3.8 %copy.25 = bf16[128,2,1,2048]{3,1,0,2:T(2,128)(2,1)} copy(bf16[128,2,1,2048]{0,1,3,2:T(2,128)(2,1)S(1)} %bitcast.43) | data formatting | bytes 2097152 | tf_op jit(solution)/shard_map/transpose | solution.py:99
  15.6 6.5 %all_to_all.27 = bf16[256,1,2048]{2,1,0:T(2,128)(2,1)S(1)} reshape(bf16[128,2,1,2048]{3,1,0,2:T(2,128)(2,1)} %copy.25) | data formatting | bytes 2097152 | tf_op jit(solution)/shard_map/all_to_all | solution.py:100
  22.6 7.7 %reduce.1 = bf16[256,2048]{1,0:T(8,128)(2,1)} reduce(bf16[256,1,2048]{2,1,0:T(2,128)(2,1)S(1)} %all_to_all.27, bf16[]{:T(256)} %broadcast.151), dimensions={1}, to_apply=%all_to_all.27.reduce_sub_computation | reduce | bytes 2097154 | tf_op jit(solution)/shard_map/all_to_all | solution.py:100
  30.3 2.6 %reshape.169 = bf16[256,2,1024]{2,1,0:T(2,128)(2,1)} reshape(bf16[256,2048]{1,0:T(8,128)(2,1)} %reduce.1) | data formatting | bytes 2097152
  32.9 14.4 %all-to-all-start.1 = ((bf16[256,2,1024]{2,1,0:T(2,128)(2,1)}), bf16[256,2,1024]{2,1,0:T(2,128)(2,1)S(1)}, u32[]{:S(2)}, u32[]{:S(2)}) async-start(bf16[256,2,1024]{2,1,0:T(2,128)(2,1)} %reshape.169), calls=%async_computation.1 | async-start | bytes 2097152 | tf_op jit(solution)/shard_map/all_to_all | solution.py:100
  47.6 1.1 copy.22
  48.7 29.2 %all-to-all-done.1 = bf16[256,2,1024]{2,1,0:T(2,128)(2,1)S(1)} async-done(((bf16[256,2,1024]{2,1,0:T(2,128)(2,1)}), bf16[256,2,1024]{2,1,0:T(2,128)(2,1)S(1)}, u32[]{:S(2)}, u32[]{:S(2)}) %all-to-all-start.1) | async-done | bytes 1048608 | tf_op jit(solution)/shard_map/all_to_all | solution.py:100
  77.9 3.6 %all-to-all-start = ((bf16[2,128,2048]{1,2,0:T(8,128)(2,1)}), bf16[2,128,2048]{1,2,0:T(8,128)(2,1)S(1)}, u32[]{:S(2)}, u32[]{:S(2)}) async-start(bf16[2,128,2048]{1,2,0:T(8,128)(2,1)} %copy.22), calls=%async_computation | async-start | bytes 2097152 | tf_op jit(solution)/shard_map/all_to_all | solution.py:89
  81.8 6.6 %reshape.170 = bf16[256,1,2048]{2,1,0:T(2,128)(2,1)S(1)} reshape(bf16[256,2,1024]{2,1,0:T(2,128)(2,1)} %copy-done.2) | data formatting | bytes 2097152
  88.4 7.2 %reduce = bf16[256,2048]{1,0:T(8,128)(2,1)} reduce(bf16[256,1,2048]{2,1,0:T(2,128)(2,1)S(1)} %reshape.170, bf16[]{:T(256)} %constant.34), dimensions={1}, to_apply=%all_to_all.25.reduce_sub_computation | reduce | bytes 2097154 | tf_op jit(solution)/shard_map/all_to_all | solution.py:100
  95.6 9.9 %reshape.156 = bf16[128,2,1,32,2,32]{5,4,3,1,0,2:T(2,128)(2,1)} reshape(bf16[256,2048]{1,0:T(8,128)(2,1)} %reduce) | data formatting | bytes 2097152 | tf_op jit(solution)/shard_map/reshape | solution.py:101
  105.5 7.0 %copy.27 = bf16[128,1,32,2,2,32]{0,5,4,3,2,1:T(8,128)(2,1)S(1)} copy(bf16[128,1,32,2,2,32]{2,3,5,4,0,1:T(2,128)(2,1)} %bitcast.37) | data formatting | bytes 2097152 | tf_op jit(solution)/shard_map/transpose | solution.py:102
  112.5 1.0 copy.29
  113.5 3.2 %gather_fusion = bf16[384,32,128]{2,1,0:T(8,128)(2,1)} fusion(bf16[128,32,128]{2,1,0:T(8,128)(2,1)S(1)} %copy.29, s32[1024]{0:T(1024)S(1)} %pad_clamp_fusion), kind=kCustom, calls=%fused_computation | custom fusion | bytes 6292992 | tf_op jit(solution)/shard_map/jit(_take)/gather | solution.py:104
  116.7 1.0 copy-done.1
  117.7 7.5 %all-to-all-start.2 = ((bf16[128,96,128]{2,1,0:T(8,128)(2,1)}), bf16[128,96,128]{2,1,0:T(8,128)(2,1)S(1)}, u32[]{:S(2)}, u32[]{:S(2)}) async-start(bf16[128,96,128]{2,1,0:T(8,128)(2,1)} %bitcast.39), calls=%async_computation.2 | async-start | bytes 6291456 | tf_op jit(solution)/shard_map/all_to_all | solution.py:107
  125.2 7.3 %copy.23 = bf16[128,2,64,32]{3,2,1,0:T(8,128)(2,1)} copy(bf16[128,2,64,32]{0,3,1,2:T(8,128)(2,1)} %bitcast.41) | data formatting | bytes 2097152 | tf_op jit(solution)/shard_map/transpose | solution.py:95
  132.5 68.4 %all-to-all-done.2 = bf16[128,96,128]{2,1,0:T(8,128)(2,1)S(1)} async-done(((bf16[128,96,128]{2,1,0:T(8,128)(2,1)}), bf16[128,96,128]{2,1,0:T(8,128)(2,1)S(1)}, u32[]{:S(2)}, u32[]{:S(2)}) %all-to-all-start.2) | async-done | bytes 3145760 | tf_op jit(solution)/shard_map/all_to_all | solution.py:107
  200.9 1.7 copy-done
  202.6 9.7 %shard_map.28 = bf16[3,128,64,128]{3,2,1,0:T(8,128)(2,1)} custom-call(bf16[128,128,32]{2,1,0:T(8,128)(2,1)} %bitcast.38, bf16[128,3,32,128]{3,2,1,0:T(8,128)(2,1)} %bitcast.40), custom_call_target="tpu_custom_call" | custom-call | tf_op jit(solution)/shard_map/pallas_call | solution.py:70
  (21 shorter events, 2.5 us)
Async XLA Ops:
  32.9 45.0 %all-to-all-start.1 = ((bf16[256,2,1024]{2,1,0:T(2,128)(2,1)}), bf16[256,2,1024]{2,1,0:T(2,128)(2,1)S(1)}, u32[]{:S(2)}, u32[]{:S(2)}) async-start(bf16[256,2,1024]{2,1,0:T(2,128)(2,1)} %reshape.169), calls=%async_computation.1 | async-start | bytes 2097152 | tf_op jit(solution)/shard_map/all_to_all | solution.py:100
  47.6 33.9 %copy-start.3 = (s32[3,128]{1,0:T(4,128)S(1)}, s32[3,128]{1,0:T(4,128)}, u32[]{:S(2)}) copy-start(s32[3,128]{1,0:T(4,128)} %param.3) | copy-start | bytes 4612
  77.9 3.9 %copy-start.2 = (bf16[256,2,1024]{2,1,0:T(2,128)(2,1)}, bf16[256,2,1024]{2,1,0:T(2,128)(2,1)S(1)}, u32[]{:S(2)}) copy-start(bf16[256,2,1024]{2,1,0:T(2,128)(2,1)S(1)} %all-to-all-done.1) | copy-start | bytes 3145732
  77.9 38.8 %all-to-all-start = ((bf16[2,128,2048]{1,2,0:T(8,128)(2,1)}), bf16[2,128,2048]{1,2,0:T(8,128)(2,1)S(1)}, u32[]{:S(2)}, u32[]{:S(2)}) async-start(bf16[2,128,2048]{1,2,0:T(8,128)(2,1)} %copy.22), calls=%async_computation | async-start | bytes 2097152 | tf_op jit(solution)/shard_map/all_to_all | solution.py:89
  116.7 1.0 copy-start.1
  117.7 83.2 %all-to-all-start.2 = ((bf16[128,96,128]{2,1,0:T(8,128)(2,1)}), bf16[128,96,128]{2,1,0:T(8,128)(2,1)S(1)}, u32[]{:S(2)}, u32[]{:S(2)}) async-start(bf16[128,96,128]{2,1,0:T(8,128)(2,1)} %bitcast.39), calls=%async_computation.2 | async-start | bytes 6291456 | tf_op jit(solution)/shard_map/all_to_all | solution.py:107
  200.9 1.7 copy-start

commit v6 on v4

--- a/solution.py
+++ b/solution.py
@@ -86,10 +86,18 @@
     spectra = whiten(raw, F)
     n_bin, half_ch, two, seg_count = spectra.shape
     norm_scale = 1.0 / math.sqrt(seg_count)
-    halves = lax.all_to_all(
-        spectra.reshape(n_bin, half_ch * two * seg_count), "grp", split_axis=0, concat_axis=1, tiled=True
+    g = lax.axis_index("grp")
+    own_bins = n_bin // n_grp
+    by_grp = spectra.reshape(n_grp, own_bins, half_ch * two * seg_count)
+    mine = lax.dynamic_index_in_dim(by_grp, g, 0, keepdims=False)
+    theirs = lax.ppermute(
+        lax.dynamic_index_in_dim(by_grp, 1 - g, 0, keepdims=False),
+        "grp",
+        [(i, (i + 1) % n_grp) for i in range(n_grp)],
     )
-    own_bins = halves.shape[0]
+    first = jnp.where(g == 0, mine, theirs)
+    second = jnp.where(g == 0, theirs, mine)
+    halves = jnp.stack([first, second], axis=1)
     block_ch = n_grp * half_ch
     halves = halves.reshape(own_bins, block_ch, two, seg_count)
     own = jnp.transpose(halves, (0, 2, 1, 3)).reshape(own_bins, two * block_ch, seg_count)

time: 175 us -> 177 us (1.011)
  blocking collectives: 16.3 us -> 0 us
  waiting for transfers between devices: 99 us -> 111 us
  local copies, waits for them, and re-layouts: 18.7 us -> 22.9 us
    all_to_all x1 -> x0, blocking collectives: 16.3 us -> none  [per_device(): lax.all_to_all(spectra.reshape(n_bin, half_ch * two * seg_count), 'grp',...]
    ppermute x0 -> x1, waiting for transfers between devices: none -> 11.6 us  [per_device(): lax.ppermute(lax.dynamic_index_in_dim(by_grp, 1 - g, 0, keepdims=False),...]
    dynamic_slice x0 -> x3, local copies, waits for them, and re-layouts: none -> 4.68 us  [the longest x2 2.88 us: per_device(): mine = lax.dynamic_index_in_dim(by_grp, g, 0, keepdims=False)]
  transfers between devices with their start and end apart: 2 -> 3, of which waited for: 2 -> 3; matrix products, arithmetic and copies ran while one was open for 4% -> 5% of each run, Pallas kernels for 0% -> 0%
where the time goes in v6:
time: 177 us; the launch traced here: 176 us
  waiting for transfers between devices  111 us (63%)
  starting transfers between devices  23.6 us (13%)
  local copies, waits for them, and re-layouts  22.9 us (13%)
  Pallas kernels  9.71 us (5%)
  matrix products  6.69 us (4%)
  other arithmetic  2.42 us (1%)
    all_to_all x1, waiting for transfers between devices, per_device(): lax.all_to_all(gathered, 'blk', split_axis=0, concat_axis=0, tiled=True)  68.4 us
    all_to_all x1, waiting for transfers between devices, per_device(): lax.all_to_all(halves.reshape(n_blk, per_owner * seg_count, width), 'blk'...  30.6 us
    all_to_all x1, starting transfers between devices, per_device(): lax.all_to_all(halves.reshape(n_blk, per_owner * seg_count, width), 'blk'...  15 us
    ppermute x1, waiting for transfers between devices, per_device(): lax.ppermute(lax.dynamic_index_in_dim(by_grp, 1 - g, 0, keepdims=False),...  11.6 us
    pallas_call x1, Pallas kernels, cross(): pl.pallas_call(lambda *refs: cross_kernel(scale, *refs), grid=(own_bins /...  9.71 us
    transpose x1, local copies, waits for them, and re-layouts, per_device(): jnp.transpose(halves, (0, 2, 1, 3))  7.29 us
    all_to_all x1, starting transfers between devices, per_device(): lax.all_to_all(gathered, 'blk', split_axis=0, concat_axis=0, tiled=True)  7.04 us
    dot_general x1, matrix products, whiten(): jnp.dot(samples.reshape(seg_count * chan_count, length), dft_table(length...  6.69 us
  transfers between devices with their start and end apart: 3, of which 3 were waited for; matrix products, arithmetic and copies ran while one was open for 5% of the time, Pallas kernels for 0%

profile of v6, /device:TPU:32, one launch (start us, length us, event | category | flops | bytes accessed | tf_op | source)
XLA Modules:
  0.0 176.2 jit_solution(11462166257155166930)
XLA Ops:
  0.0 0.2 fusion.23
  0.2 0.3 fusion.16
  0.6 1.2 subtract_convert_fusion
  1.7 6.7 %fusion.4 = f32[1024,512]{0,1:T(8,128)} fusion(bf16[1024,2400]{1,0:T(8,128)(2,1)} %bitcast.50, bf16[2400,256]{1,0:T(8,128)(2,1)S(1)} %bitcast.48, bf16[2400,256]{1,0:T(8,128)(2,1)S(1)} %bitcast.47), kind=kOutput, calls=%fused_computation.7 | convolution fusion | flops 2521497600 | bytes 9469952 | tf_op jit(solution)/shard_map/dot_general | solution.py:37
  8.4 1.9 %copy.8 = f32[1024,512]{1,0:T(8,128)S(1)} copy(f32[1024,512]{0,1:T(8,128)} %fusion.4) | data formatting | bytes 4194304 | tf_op jit(solution)/shard_map/dot_general | solution.py:37
  10.5 0.3 fusion.7
  10.9 0.6 copy.9
  11.5 0.3 reshape.139
  11.8 2.2 %constant_dynamic-slice_fusion.1 = (bf16[1,128,2048]{1,0,2:T(2,128)(2,1)S(1)}, bf16[1,128,2048]{1,0,2:T(2,128)(2,1)S(1)}) fusion(bf16[2,128,2048]{1,0,2:T(2,128)(2,1)S(1)} %reshape.139, s32[]{:T(128)S(6)} %select_n.53, s32[]{:T(128)S(6)} %select_n.54), kind=kLoop, calls=%fused_computation.42 | loop fusion | bytes 2097160 | tf_op jit(solution)/shard_map/jit(dynamic_index_in_dim)/dynamic_slice | solution.py:92
  14.0 1.8 %copy.11 = bf16[1,128,2048]{2,1,0:T(8,128)(2,1)} copy(bf16[1,128,2048]{1,0,2:T(2,128)(2,1)S(1)} %get-tuple-element.10) | data formatting | bytes 1048576 | tf_op jit(solution)/shard_map/jit(dynamic_index_in_dim)/dynamic_slice | solution.py:94
  15.8 1.6 collective-permute-start
  17.4 0.7 copy.10
  18.1 11.6 %collective-permute-done = bf16[128,2048]{1,0:T(8,128)(2,1)S(1)} collective-permute-done((bf16[128,2048]{1,0:T(8,128)(2,1)}, bf16[128,2048]{1,0:T(8,128)(2,1)S(1)}, u32[]{:S(2)}, u32[]{:S(2)}) %collective-permute-start) | collective-permute-done | bytes 524320 | tf_op jit(solution)/shard_map/ppermute | solution.py:93
  29.9 0.7 copy.12
  30.6 0.7 copy.14
  31.3 1.7 copy.15
  32.9 15.0 %all-to-all-start = ((bf16[128,32,128]{2,1,0:T(8,128)(2,1)}), bf16[128,32,128]{2,1,0:T(8,128)(2,1)S(1)}, u32[]{:S(2)}, u32[]{:S(2)}) async-start(bf16[128,32,128]{2,1,0:T(8,128)(2,1)} %copy.15), calls=%async_computation | async-start | bytes 2097152 | tf_op jit(solution)/shard_map/all_to_all | solution.py:107
  48.3 30.6 %all-to-all-done = bf16[128,32,128]{2,1,0:T(8,128)(2,1)S(1)} async-done(((bf16[128,32,128]{2,1,0:T(8,128)(2,1)}), bf16[128,32,128]{2,1,0:T(8,128)(2,1)S(1)}, u32[]{:S(2)}, u32[]{:S(2)}) %all-to-all-start) | async-done | bytes 1048608 | tf_op jit(solution)/shard_map/all_to_all | solution.py:107
  78.9 3.2 %gather_fusion = bf16[384,32,128]{2,1,0:T(8,128)(2,1)} fusion(bf16[128,32,128]{2,1,0:T(8,128)(2,1)S(1)} %all-to-all-done, s32[1024]{0:T(1024)S(1)} %pad_clamp_fusion), kind=kCustom, calls=%fused_computation | custom fusion | bytes 6292992 | tf_op jit(solution)/shard_map/jit(_take)/gather | solution.py:111
  82.1 7.0 %all-to-all-start.1 = ((bf16[128,96,128]{2,1,0:T(8,128)(2,1)}), bf16[128,96,128]{2,1,0:T(8,128)(2,1)S(1)}, u32[]{:S(2)}, u32[]{:S(2)}) async-start(bf16[128,96,128]{2,1,0:T(8,128)(2,1)} %bitcast.42), calls=%async_computation.1 | async-start | bytes 6291456 | tf_op jit(solution)/shard_map/all_to_all | solution.py:114
  89.1 7.3 %copy.13 = bf16[128,2,64,32]{3,2,1,0:T(8,128)(2,1)} copy(bf16[128,2,64,32]{0,3,1,2:T(8,128)(2,1)} %bitcast.45) | data formatting | bytes 2097152 | tf_op jit(solution)/shard_map/transpose | solution.py:103
  96.4 68.4 %all-to-all-done.1 = bf16[128,96,128]{2,1,0:T(8,128)(2,1)S(1)} async-done(((bf16[128,96,128]{2,1,0:T(8,128)(2,1)}), bf16[128,96,128]{2,1,0:T(8,128)(2,1)S(1)}, u32[]{:S(2)}, u32[]{:S(2)}) %all-to-all-start.1) | async-done | bytes 3145760 | tf_op jit(solution)/shard_map/all_to_all | solution.py:114
  164.8 1.7 copy-done
  166.5 9.7 %shard_map.28 = bf16[3,128,64,128]{3,2,1,0:T(8,128)(2,1)} custom-call(bf16[128,128,32]{2,1,0:T(8,128)(2,1)} %bitcast.41, bf16[128,3,32,128]{3,2,1,0:T(8,128)(2,1)} %bitcast.43), custom_call_target="tpu_custom_call" | custom-call | tf_op jit(solution)/shard_map/pallas_call | solution.py:70
  (15 shorter events, 0.8 us)
Async XLA Ops:
  15.8 13.9 %collective-permute-start = (bf16[128,2048]{1,0:T(8,128)(2,1)}, bf16[128,2048]{1,0:T(8,128)(2,1)S(1)}, u32[]{:S(2)}, u32[]{:S(2)}) collective-permute-start(bf16[128,2048]{1,0:T(8,128)(2,1)} %bitcast.9), channel_id=1, source_target_pairs={{0,1},{1,0},{2,3},{3,2},{4,5},{5,4},{6,7},{7,6},{8,9},{9,8},{10,11... | collective-permute-start | bytes 1572872 | tf_op jit(solution)/shard_map/ppermute | solution.py:93
  30.6 2.4 %copy-start.1 = (bf16[128,2,2048]{0,2,1:T(8,128)(2,1)}, bf16[128,2,2048]{0,2,1:T(8,128)(2,1)S(1)}, u32[]{:S(2)}) copy-start(bf16[128,2,2048]{0,2,1:T(8,128)(2,1)S(1)} %copy.12) | copy-start | bytes 3145732
  31.3 16.7 %copy-start.2 = (s32[3,128]{1,0:T(4,128)S(1)}, s32[3,128]{1,0:T(4,128)}, u32[]{:S(2)}) copy-start(s32[3,128]{1,0:T(4,128)} %param.3) | copy-start | bytes 4612
  32.9 46.0 %all-to-all-start = ((bf16[128,32,128]{2,1,0:T(8,128)(2,1)}), bf16[128,32,128]{2,1,0:T(8,128)(2,1)S(1)}, u32[]{:S(2)}, u32[]{:S(2)}) async-start(bf16[128,32,128]{2,1,0:T(8,128)(2,1)} %copy.15), calls=%async_computation | async-start | bytes 2097152 | tf_op jit(solution)/shard_map/all_to_all | solution.py:107
  82.1 82.8 %all-to-all-start.1 = ((bf16[128,96,128]{2,1,0:T(8,128)(2,1)}), bf16[128,96,128]{2,1,0:T(8,128)(2,1)S(1)}, u32[]{:S(2)}, u32[]{:S(2)}) async-start(bf16[128,96,128]{2,1,0:T(8,128)(2,1)} %bitcast.42), calls=%async_computation.1 | async-start | bytes 6291456 | tf_op jit(solution)/shard_map/all_to_all | solution.py:114
  164.8 1.7 copy-start

commit v7 on v4

--- a/solution.py
+++ b/solution.py
@@ -53,11 +53,11 @@
     lane = lax.broadcasted_iota(jnp.int32, (block_ch, width), 1)
     sign = jnp.where(lane < width // 2, scale, -scale).astype(jnp.float32)
     for f in range(bins):
-        a = a_ref[f]
+        rhs = jnp.concatenate([rec_ref[f, r] for r in range(rounds)], axis=1)
+        both = jnp.dot(a_ref[f], rhs, preferred_element_type=jnp.float32)
         for r in range(rounds):
-            both = jnp.dot(a, rec_ref[f, r], preferred_element_type=jnp.float32)
-            p1 = both[:block_ch]
-            p2 = both[block_ch:]
+            p1 = both[:block_ch, r * width:(r + 1) * width]
+            p2 = both[block_ch:, r * width:(r + 1) * width]
             out = pltpu.roll(p2, width // 2, 1) * scale + p1 * sign
             out_ref[r, f] = out.astype(out_ref.dtype)
 
@@ -66,7 +66,7 @@
     own_bins, two_ch, seg_count = a.shape
     rounds, width = rec.shape[1], rec.shape[-1]
     block_ch = two_ch // 2
-    fb = 16
+    fb = 32
     return pl.pallas_call(
         lambda *refs: cross_kernel(scale, *refs),
         grid=(own_bins // fb,),

time: 175 us -> 173 us (0.989)
  Pallas kernels: 9.71 us -> 7.91 us
    pallas_call x1, Pallas kernels: 9.71 us -> 7.91 us  [cross(): pl.pallas_call(lambda *refs: cross_kernel(scale, *refs), grid=(own_bins /...]
where the time goes in v7:
time: 173 us
  waiting for transfers between devices  99 us (57%)
  starting transfers between devices  22 us (13%)
  local copies, waits for them, and re-layouts  18.7 us (11%)
  blocking collectives  16.3 us (9%)
  Pallas kernels  7.91 us (5%)
  matrix products  6.69 us (4%)
  other arithmetic  2.25 us (1%)
    all_to_all x1, waiting for transfers between devices, per_device(): lax.all_to_all(gathered, 'blk', split_axis=0, concat_axis=0, tiled=True)  68.4 us
    all_to_all x1, waiting for transfers between devices, per_device(): lax.all_to_all(halves.reshape(n_blk, per_owner * seg_count, width), 'blk'...  30.6 us
    all_to_all x1, blocking collectives, per_device(): lax.all_to_all(spectra.reshape(n_bin, half_ch * two * seg_count), 'grp',...  16.3 us
    all_to_all x1, starting transfers between devices, per_device(): lax.all_to_all(halves.reshape(n_blk, per_owner * seg_count, width), 'blk'...  15 us
    pallas_call x1, Pallas kernels, cross(): pl.pallas_call(lambda *refs: cross_kernel(scale, *refs), grid=(own_bins /...  7.91 us
    transpose x1, local copies, waits for them, and re-layouts, per_device(): jnp.transpose(halves, (0, 2, 1, 3))  7.31 us
    all_to_all x1, starting transfers between devices, per_device(): lax.all_to_all(gathered, 'blk', split_axis=0, concat_axis=0, tiled=True)  7.04 us
    dot_general x1, matrix products, whiten(): jnp.dot(samples.reshape(seg_count * chan_count, length), dft_table(length...  6.69 us
  transfers between devices with their start and end apart: 2, of which 2 were waited for; matrix products, arithmetic and copies ran while one was open for 4% of the time, Pallas kernels for 0%

profile of v7, /device:TPU:32, one launch (start us, length us, event | category | flops | bytes accessed | tf_op | source)
XLA Modules:
  0.0 173.1 jit_solution(14627441309126885666)
XLA Ops:
  0.0 0.2 fusion.21
  0.2 0.3 fusion.14
  0.6 1.2 subtract_convert_fusion
  1.7 6.7 %fusion.4 = f32[1024,512]{0,1:T(8,128)} fusion(bf16[1024,2400]{1,0:T(8,128)(2,1)} %bitcast.40, bf16[2400,256]{1,0:T(8,128)(2,1)S(1)} %bitcast.38, bf16[2400,256]{1,0:T(8,128)(2,1)S(1)} %bitcast.37), kind=kOutput, calls=%fused_computation.7 | convolution fusion | flops 2521497600 | bytes 9469952 | tf_op jit(solution)/shard_map/dot_general | solution.py:37
  8.4 1.9 %copy.16 = f32[1024,512]{1,0:T(8,128)S(1)} copy(f32[1024,512]{0,1:T(8,128)} %fusion.4) | data formatting | bytes 4194304 | tf_op jit(solution)/shard_map/dot_general | solution.py:37
  10.3 0.1 add_reduce_fusion
  10.5 0.3 fusion.7
  10.9 0.6 copy.17
  11.5 0.3 all_to_all.18
  11.8 0.1 copy.18
  11.9 16.3 %all_to_all.26 = bf16[2,128,2048]{1,2,0:T(8,128)(2,1)S(1)} all-to-all(bf16[2,128,2048]{1,2,0:T(8,128)(2,1)S(1)} %copy.18), channel_id=1, replica_groups=mesh['blk'=128,'grp'=2] {'grp'}, dimensions={0} | all-to-all | bytes 2097152 | tf_op jit(solution)/shard_map/all_to_all | solution.py:89
  28.3 1.0 copy-done.1
  29.2 0.7 copy.20
  29.9 1.7 copy.21
  31.6 15.0 %all-to-all-start.1 = ((bf16[128,32,128]{2,1,0:T(8,128)(2,1)}), bf16[128,32,128]{2,1,0:T(8,128)(2,1)S(1)}, u32[]{:S(2)}, u32[]{:S(2)}) async-start(bf16[128,32,128]{2,1,0:T(8,128)(2,1)} %copy.21), calls=%async_computation.1 | async-start | bytes 2097152 | tf_op jit(solution)/shard_map/all_to_all | solution.py:99
  46.6 0.1 copy.22
  46.7 0.2 reshape.148
  47.0 30.6 %all-to-all-done.1 = bf16[128,32,128]{2,1,0:T(8,128)(2,1)S(1)} async-done(((bf16[128,32,128]{2,1,0:T(8,128)(2,1)}), bf16[128,32,128]{2,1,0:T(8,128)(2,1)S(1)}, u32[]{:S(2)}, u32[]{:S(2)}) %all-to-all-start.1) | async-done | bytes 1048608 | tf_op jit(solution)/shard_map/all_to_all | solution.py:99
  77.6 3.2 %gather_fusion = bf16[384,32,128]{2,1,0:T(8,128)(2,1)} fusion(bf16[128,32,128]{2,1,0:T(8,128)(2,1)S(1)} %all-to-all-done.1, s32[1024]{0:T(1024)S(1)} %pad_clamp_fusion), kind=kCustom, calls=%fused_computation | custom fusion | bytes 6292992 | tf_op jit(solution)/shard_map/jit(_take)/gather | solution.py:103
  80.7 7.0 %all-to-all-start.2 = ((bf16[128,96,128]{2,1,0:T(8,128)(2,1)}), bf16[128,96,128]{2,1,0:T(8,128)(2,1)S(1)}, u32[]{:S(2)}, u32[]{:S(2)}) async-start(bf16[128,96,128]{2,1,0:T(8,128)(2,1)} %bitcast.32), calls=%async_computation.2 | async-start | bytes 6291456 | tf_op jit(solution)/shard_map/all_to_all | solution.py:106
  87.8 7.3 %copy.19 = bf16[128,2,64,32]{3,2,1,0:T(8,128)(2,1)} copy(bf16[128,2,64,32]{0,3,1,2:T(8,128)(2,1)} %bitcast.35) | data formatting | bytes 2097152 | tf_op jit(solution)/shard_map/transpose | solution.py:95
  95.1 68.4 %all-to-all-done.2 = bf16[128,96,128]{2,1,0:T(8,128)(2,1)S(1)} async-done(((bf16[128,96,128]{2,1,0:T(8,128)(2,1)}), bf16[128,96,128]{2,1,0:T(8,128)(2,1)S(1)}, u32[]{:S(2)}, u32[]{:S(2)}) %all-to-all-start.2) | async-done | bytes 3145760 | tf_op jit(solution)/shard_map/all_to_all | solution.py:106
  163.5 1.7 copy-done
  165.1 7.9 %shard_map.28 = bf16[3,128,64,128]{3,2,1,0:T(8,128)(2,1)} custom-call(bf16[128,128,32]{2,1,0:T(8,128)(2,1)} %bitcast.31, bf16[128,3,32,128]{3,2,1,0:T(8,128)(2,1)} %bitcast.33), custom_call_target="tpu_custom_call" | custom-call | tf_op jit(solution)/shard_map/pallas_call | solution.py:70
  (9 shorter events, 0.1 us)
Async XLA Ops:
  28.3 1.0 copy-start.1
  29.9 16.7 %copy-start.2 = (s32[3,128]{1,0:T(4,128)S(1)}, s32[3,128]{1,0:T(4,128)}, u32[]{:S(2)}) copy-start(s32[3,128]{1,0:T(4,128)} %param.3) | copy-start | bytes 4612
  31.6 45.9 %all-to-all-start.1 = ((bf16[128,32,128]{2,1,0:T(8,128)(2,1)}), bf16[128,32,128]{2,1,0:T(8,128)(2,1)S(1)}, u32[]{:S(2)}, u32[]{:S(2)}) async-start(bf16[128,32,128]{2,1,0:T(8,128)(2,1)} %copy.21), calls=%async_computation.1 | async-start | bytes 2097152 | tf_op jit(solution)/shard_map/all_to_all | solution.py:99
  80.7 82.8 %all-to-all-start.2 = ((bf16[128,96,128]{2,1,0:T(8,128)(2,1)}), bf16[128,96,128]{2,1,0:T(8,128)(2,1)S(1)}, u32[]{:S(2)}, u32[]{:S(2)}) async-start(bf16[128,96,128]{2,1,0:T(8,128)(2,1)} %bitcast.32), calls=%async_computation.2 | async-start | bytes 6291456 | tf_op jit(solution)/shard_map/all_to_all | solution.py:106
  163.5 1.7 copy-start

commit v8 on v7

--- a/solution.py
+++ b/solution.py
@@ -15,28 +15,28 @@
 epsilon = 1e-06
 
 
-def phase_table(step, rows, num_bins, length):
+def phase_table(step, rows, num_bins, length, base):
     sample_idx = lax.broadcasted_iota(jnp.int32, (rows, num_bins), 0) * step
-    bin_index = lax.broadcasted_iota(jnp.int32, (rows, num_bins), 1) + first_bin
+    bin_index = lax.broadcasted_iota(jnp.int32, (rows, num_bins), 1) + (first_bin + base)
     phase_angle = (sample_idx * bin_index % length).astype(jnp.float32) * (2.0 * math.pi / length)
     return jnp.cos(phase_angle), jnp.sin(phase_angle)
 
 
-def dft_table(length, num_bins):
+def dft_table(length, num_bins, base):
     step = 48 if length % 48 == 0 else 1
-    cos_c, sin_c = phase_table(step, length // step, num_bins, length)
-    cos_f, sin_f = phase_table(1, step, num_bins, length)
+    cos_c, sin_c = phase_table(step, length // step, num_bins, length, base)
+    cos_f, sin_f = phase_table(1, step, num_bins, length, base)
     cos_t = cos_c[:, None] * cos_f[None] - sin_c[:, None] * sin_f[None]
     sin_t = sin_c[:, None] * cos_f[None] + cos_c[:, None] * sin_f[None]
     table = jnp.concatenate([cos_t, -sin_t], axis=-1).reshape(length, 2 * num_bins)
     return table.astype(jnp.bfloat16)
 
 
-def whiten(samples, num_bins):
+def whiten(samples, num_bins, base):
     seg_count, chan_count, length = samples.shape
     spectrum = jnp.dot(
         samples.reshape(seg_count * chan_count, length),
-        dft_table(length, num_bins),
+        dft_table(length, num_bins, base),
         preferred_element_type=jnp.float32,
     ).reshape(seg_count, chan_count, 2 * num_bins)
     real_part = spectrum[:, :, :num_bins]
@@ -83,12 +83,20 @@
 def per_device(raw, partner):
     n_blk = lax.axis_size("blk")
     n_grp = lax.axis_size("grp")
-    spectra = whiten(raw, F)
-    n_bin, half_ch, two, seg_count = spectra.shape
+    g = lax.axis_index("grp")
+    own_bins = F // n_grp
+    sent = whiten(raw, own_bins, (1 - g) * own_bins)
+    half_ch, two, seg_count = sent.shape[1:]
     norm_scale = 1.0 / math.sqrt(seg_count)
-    halves = lax.all_to_all(
-        spectra.reshape(n_bin, half_ch * two * seg_count), "grp", split_axis=0, concat_axis=1, tiled=True
+    theirs = lax.ppermute(
+        sent.reshape(own_bins, half_ch * two * seg_count),
+        "grp",
+        [(i, (i + 1) % n_grp) for i in range(n_grp)],
     )
+    mine = whiten(raw, own_bins, g * own_bins).reshape(own_bins, half_ch * two * seg_count)
+    first = jnp.where(g == 0, mine, theirs)
+    second = jnp.where(g == 0, theirs, mine)
+    halves = jnp.stack([first, second], axis=1)
     own_bins = halves.shape[0]
     block_ch = n_grp * half_ch
     halves = halves.reshape(own_bins, block_ch, two, seg_count)

time: 173 us -> 167 us (0.965)
  blocking collectives: 16.3 us -> 0 us
  waiting for transfers between devices: 99 us -> 107 us
  starting transfers between devices: 22 us -> 23.8 us
    all_to_all x1 -> x0, blocking collectives: 16.3 us -> none  [per_device(): lax.all_to_all(spectra.reshape(n_bin, half_ch * two * seg_count), 'grp',...]
    ppermute x0 -> x1, waiting for transfers between devices: none -> 7.59 us  [per_device(): lax.ppermute(sent.reshape(own_bins, half_ch * two * seg_count), 'grp', [(...]
    dot_general x1 -> x2, matrix products: 6.69 us -> 7.99 us  [whiten(): jnp.dot(samples.reshape(seg_count * chan_count, length), dft_table(length...]
  transfers between devices with their start and end apart: 2 -> 3, of which waited for: 2 -> 3; matrix products, arithmetic and copies ran while one was open for 4% -> 7% of each run, Pallas kernels for 0% -> 0%
where the time goes in v8:
time: 167 us
  waiting for transfers between devices  107 us (64%)
  starting transfers between devices  23.8 us (14%)
  local copies, waits for them, and re-layouts  17.6 us (11%)
  matrix products  7.99 us (5%)
  Pallas kernels  7.9 us (5%)
  other arithmetic  2.99 us (2%)
    all_to_all x1, waiting for transfers between devices, per_device(): lax.all_to_all(gathered, 'blk', split_axis=0, concat_axis=0, tiled=True)  68.4 us
    all_to_all x1, waiting for transfers between devices, per_device(): lax.all_to_all(halves.reshape(n_blk, per_owner * seg_count, width), 'blk'...  30.6 us
    all_to_all x1, starting transfers between devices, per_device(): lax.all_to_all(halves.reshape(n_blk, per_owner * seg_count, width), 'blk'...  15.1 us
    dot_general x2, matrix products, whiten(): jnp.dot(samples.reshape(seg_count * chan_count, length), dft_table(length...  7.99 us
    pallas_call x1, Pallas kernels, cross(): pl.pallas_call(lambda *refs: cross_kernel(scale, *refs), grid=(own_bins /...  7.9 us
    ppermute x1, waiting for transfers between devices, per_device(): lax.ppermute(sent.reshape(own_bins, half_ch * two * seg_count), 'grp', [(...  7.59 us
    transpose x1, local copies, waits for them, and re-layouts, per_device(): jnp.transpose(halves, (0, 2, 1, 3))  7.3 us
    all_to_all x1, starting transfers between devices, per_device(): lax.all_to_all(gathered, 'blk', split_axis=0, concat_axis=0, tiled=True)  7.04 us
  transfers between devices with their start and end apart: 3, of which 3 were waited for; matrix products, arithmetic and copies ran while one was open for 7% of the time, Pallas kernels for 0%

profile of v8, /device:TPU:32, one launch (start us, length us, event | category | flops | bytes accessed | tf_op | source)
XLA Modules:
  0.0 167.0 jit_solution(9807799922103339136)
XLA Ops:
  0.0 0.1 fusion.31
  0.3 0.3 fusion.21
  0.6 0.7 subtract_convert_fusion
  1.3 4.0 %convolution_bitcast_fusion = f32[1024,256]{0,1:T(8,128)S(1)} fusion(bf16[1024,2400]{1,0:T(8,128)(2,1)} %bitcast.58, bf16[2400,128]{1,0:T(8,128)(2,1)S(1)} %bitcast.56, bf16[2400,128]{1,0:T(8,128)(2,1)S(1)} %bitcast.55), kind=kOutput, calls=%fused_computation.1 | convolution fusion | flops 1260748800 | bytes 7192576 | tf_op jit(solution)/shard_map/dot_general | solution.py:37
  5.3 0.3 copy.12
  5.9 1.0 copy.13
  6.9 1.6 collective-permute-start
  8.5 4.0 %convolution_bitcast_fusion.1 = f32[1024,256]{0,1:T(8,128)S(1)} fusion(bf16[1024,2400]{1,0:T(8,128)(2,1)} %bitcast.59, bf16[2400,128]{1,0:T(8,128)(2,1)S(1)} %bitcast.53, bf16[2400,128]{1,0:T(8,128)(2,1)S(1)} %bitcast.54), kind=kOutput, calls=%fused_computation.2 | convolution fusion | flops 1260748800 | bytes 7192576 | tf_op jit(solution)/shard_map/dot_general | solution.py:37
  12.5 0.3 copy.10
  13.1 0.2 copy.11
  13.3 7.6 %collective-permute-done = bf16[128,2048]{0,1:T(8,128)(2,1)} collective-permute-done((bf16[128,2048]{0,1:T(8,128)(2,1)}, bf16[128,2048]{0,1:T(8,128)(2,1)}, u32[]{:S(2)}, u32[]{:S(2)}) %collective-permute-start) | collective-permute-done | bytes 524320 | tf_op jit(solution)/shard_map/ppermute | solution.py:91
  20.9 1.1 bitcast_select_fusion.1
  22.1 1.0 copy-done.1
  23.1 0.7 copy.15
  23.8 1.7 %copy.16 = bf16[128,32,128]{2,1,0:T(8,128)(2,1)} copy(bf16[128,32,128]{0,2,1:T(8,128)(2,1)S(1)} %bitcast.50) | data formatting | bytes 2097152 | tf_op jit(solution)/shard_map/reshape | solution.py:108
  25.5 15.1 %all-to-all-start = ((bf16[128,32,128]{2,1,0:T(8,128)(2,1)}), bf16[128,32,128]{2,1,0:T(8,128)(2,1)S(1)}, u32[]{:S(2)}, u32[]{:S(2)}) async-start(bf16[128,32,128]{2,1,0:T(8,128)(2,1)} %copy.16), calls=%async_computation | async-start | bytes 2097152 | tf_op jit(solution)/shard_map/all_to_all | solution.py:107
  40.7 0.2 reshape.269
  40.9 30.6 %all-to-all-done = bf16[128,32,128]{2,1,0:T(8,128)(2,1)S(1)} async-done(((bf16[128,32,128]{2,1,0:T(8,128)(2,1)}), bf16[128,32,128]{2,1,0:T(8,128)(2,1)S(1)}, u32[]{:S(2)}, u32[]{:S(2)}) %all-to-all-start) | async-done | bytes 1048608 | tf_op jit(solution)/shard_map/all_to_all | solution.py:107
  71.5 3.2 %gather_fusion = bf16[384,32,128]{2,1,0:T(8,128)(2,1)} fusion(bf16[128,32,128]{2,1,0:T(8,128)(2,1)S(1)} %all-to-all-done, s32[1024]{0:T(1024)S(1)} %pad_clamp_fusion), kind=kCustom, calls=%fused_computation | custom fusion | bytes 6292992 | tf_op jit(solution)/shard_map/jit(_take)/gather | solution.py:111
  74.7 7.0 %all-to-all-start.1 = ((bf16[128,96,128]{2,1,0:T(8,128)(2,1)}), bf16[128,96,128]{2,1,0:T(8,128)(2,1)S(1)}, u32[]{:S(2)}, u32[]{:S(2)}) async-start(bf16[128,96,128]{2,1,0:T(8,128)(2,1)} %bitcast.42), calls=%async_computation.1 | async-start | bytes 6291456 | tf_op jit(solution)/shard_map/all_to_all | solution.py:114
  81.8 7.3 %copy.14 = bf16[128,2,64,32]{3,2,1,0:T(8,128)(2,1)} copy(bf16[128,2,64,32]{0,3,1,2:T(8,128)(2,1)} %bitcast.45) | data formatting | bytes 2097152 | tf_op jit(solution)/shard_map/transpose | solution.py:103
  89.1 68.4 %all-to-all-done.1 = bf16[128,96,128]{2,1,0:T(8,128)(2,1)S(1)} async-done(((bf16[128,96,128]{2,1,0:T(8,128)(2,1)}), bf16[128,96,128]{2,1,0:T(8,128)(2,1)S(1)}, u32[]{:S(2)}, u32[]{:S(2)}) %all-to-all-start.1) | async-done | bytes 3145760 | tf_op jit(solution)/shard_map/all_to_all | solution.py:114
  157.5 1.7 copy-done
  159.1 7.9 %shard_map.28 = bf16[3,128,64,128]{3,2,1,0:T(8,128)(2,1)} custom-call(bf16[128,128,32]{2,1,0:T(8,128)(2,1)} %bitcast.41, bf16[128,3,32,128]{3,2,1,0:T(8,128)(2,1)} %bitcast.43), custom_call_target="tpu_custom_call" | custom-call | tf_op jit(solution)/shard_map/pallas_call | solution.py:70
  (19 shorter events, 0.8 us)
Async XLA Ops:
  6.9 14.0 %collective-permute-start = (bf16[128,2048]{0,1:T(8,128)(2,1)}, bf16[128,2048]{0,1:T(8,128)(2,1)}, u32[]{:S(2)}, u32[]{:S(2)}) collective-permute-start(bf16[128,2048]{0,1:T(8,128)(2,1)} %bitcast.16), channel_id=1, source_target_pairs={{0,1},{1,0},{2,3},{3,2},{4,5},{5,4},{6,7},{7,6},{8,9},{9,8},{10,11... | collective-permute-start | bytes 1572872 | tf_op jit(solution)/shard_map/ppermute | solution.py:91
  22.1 1.0 copy-start.1
  25.4 15.1 %copy-start.2 = (s32[3,128]{1,0:T(4,128)S(1)}, s32[3,128]{1,0:T(4,128)}, u32[]{:S(2)}) copy-start(s32[3,128]{1,0:T(4,128)} %param.3) | copy-start | bytes 4612
  25.5 46.1 %all-to-all-start = ((bf16[128,32,128]{2,1,0:T(8,128)(2,1)}), bf16[128,32,128]{2,1,0:T(8,128)(2,1)S(1)}, u32[]{:S(2)}, u32[]{:S(2)}) async-start(bf16[128,32,128]{2,1,0:T(8,128)(2,1)} %copy.16), calls=%async_computation | async-start | bytes 2097152 | tf_op jit(solution)/shard_map/all_to_all | solution.py:107
  74.7 82.8 %all-to-all-start.1 = ((bf16[128,96,128]{2,1,0:T(8,128)(2,1)}), bf16[128,96,128]{2,1,0:T(8,128)(2,1)S(1)}, u32[]{:S(2)}, u32[]{:S(2)}) async-start(bf16[128,96,128]{2,1,0:T(8,128)(2,1)} %bitcast.42), calls=%async_computation.1 | async-start | bytes 6291456 | tf_op jit(solution)/shard_map/all_to_all | solution.py:114
  157.5 1.7 copy-start

commit v9 on v8

--- a/solution.py
+++ b/solution.py
@@ -85,14 +85,21 @@
     n_grp = lax.axis_size("grp")
     g = lax.axis_index("grp")
     own_bins = F // n_grp
-    sent = whiten(raw, own_bins, (1 - g) * own_bins)
-    half_ch, two, seg_count = sent.shape[1:]
+    pieces = 2 if own_bins % 2 == 0 else 1
+    piece = own_bins // pieces
+    received = []
+    for i in range(pieces):
+        sent = whiten(raw, piece, (1 - g) * own_bins + i * piece)
+        half_ch, two, seg_count = sent.shape[1:]
+        received.append(
+            lax.ppermute(
+                sent.reshape(piece, half_ch * two * seg_count),
+                "grp",
+                [(j, (j + 1) % n_grp) for j in range(n_grp)],
+            )
+        )
     norm_scale = 1.0 / math.sqrt(seg_count)
-    theirs = lax.ppermute(
-        sent.reshape(own_bins, half_ch * two * seg_count),
-        "grp",
-        [(i, (i + 1) % n_grp) for i in range(n_grp)],
-    )
+    theirs = jnp.concatenate(received, axis=0)
     mine = whiten(raw, own_bins, g * own_bins).reshape(own_bins, half_ch * two * seg_count)
     first = jnp.where(g == 0, mine, theirs)
     second = jnp.where(g == 0, theirs, mine)

time: 167 us -> 179 us (1.072)
  matrix products: 7.99 us -> 13.1 us
  waiting for transfers between devices: 107 us -> 111 us
  other arithmetic: 2.99 us -> 5.04 us
    dot_general x2 -> x3, matrix products: 7.99 us -> 13.1 us  [whiten(): jnp.dot(samples.reshape(seg_count * chan_count, length), dft_table(length...]
    ppermute x1 -> x2, waiting for transfers between devices: 7.59 us -> 11.8 us  [per_device(): lax.ppermute(sent.reshape(piece, half_ch * two * seg_count), 'grp', [(j,...]
  transfers between devices with their start and end apart: 3 -> 4, of which waited for: 3 -> 4; matrix products, arithmetic and copies ran while one was open for 7% -> 10% of each run, Pallas kernels for 0% -> 0%
where the time goes in v9:
time: 179 us
  waiting for transfers between devices  111 us (62%)
  starting transfers between devices  24.4 us (14%)
  local copies, waits for them, and re-layouts  17.1 us (10%)
  matrix products  13.1 us (7%)
  Pallas kernels  7.9 us (4%)
  other arithmetic  5.04 us (3%)
    all_to_all x1, waiting for transfers between devices, per_device(): lax.all_to_all(gathered, 'blk', split_axis=0, concat_axis=0, tiled=True)  68.4 us
    all_to_all x1, waiting for transfers between devices, per_device(): lax.all_to_all(halves.reshape(n_blk, per_owner * seg_count, width), 'blk'...  30.6 us
    all_to_all x1, starting transfers between devices, per_device(): lax.all_to_all(halves.reshape(n_blk, per_owner * seg_count, width), 'blk'...  15.1 us
    dot_general x3, matrix products, whiten(): jnp.dot(samples.reshape(seg_count * chan_count, length), dft_table(length...  13.1 us
    ppermute x2, waiting for transfers between devices, per_device(): lax.ppermute(sent.reshape(piece, half_ch * two * seg_count), 'grp', [(j,...  11.8 us
    pallas_call x1, Pallas kernels, cross(): pl.pallas_call(lambda *refs: cross_kernel(scale, *refs), grid=(own_bins /...  7.9 us
    transpose x1, local copies, waits for them, and re-layouts, per_device(): jnp.transpose(halves, (0, 2, 1, 3))  7.29 us
    all_to_all x1, starting transfers between devices, per_device(): lax.all_to_all(gathered, 'blk', split_axis=0, concat_axis=0, tiled=True)  7.04 us
  transfers between devices with their start and end apart: 4, of which 4 were waited for; matrix products, arithmetic and copies ran while one was open for 10% of the time, Pallas kernels for 0%

profile of v9, /device:TPU:32, one launch (start us, length us, event | category | flops | bytes accessed | tf_op | source)
XLA Modules:
  0.0 178.6 jit_solution(7056300765184893407)
XLA Ops:
  0.3 0.3 fusion.28
  0.6 0.7 subtract_convert_fusion
  1.3 4.6 %convolution_bitcast_fusion.2 = f32[1024,128]{0,1:T(8,128)S(1)} fusion(bf16[1024,2400]{1,0:T(8,128)(2,1)} %bitcast.52, bf16[2400,64]{1,0:T(8,128)(2,1)S(1)} %bitcast.69, bf16[2400,64]{1,0:T(8,128)(2,1)S(1)} %bitcast.70), kind=kOutput, calls=%fused_computation.3 | convolution fusion | flops 630374400 | bytes 6053888 | tf_op jit(solution)/shard_map/dot_general | solution.py:37
  6.1 0.2 add_reduce_fusion.1
  6.9 1.7 collective-permute-start
  8.5 4.6 %convolution_bitcast_fusion.1 = f32[1024,128]{0,1:T(8,128)S(1)} fusion(bf16[1024,2400]{1,0:T(8,128)(2,1)} %bitcast.53, bf16[2400,64]{1,0:T(8,128)(2,1)S(1)} %bitcast.68, bf16[2400,64]{1,0:T(8,128)(2,1)S(1)} %bitcast.67), kind=kOutput, calls=%fused_computation.2 | convolution fusion | flops 630374400 | bytes 6053888 | tf_op jit(solution)/shard_map/dot_general | solution.py:37
  14.1 0.5 collective-permute-start.1
  15.0 0.4 subtract_convert_fusion.2
  15.3 4.0 %convolution_bitcast_fusion = f32[1024,256]{0,1:T(8,128)S(1)} fusion(bf16[1024,2400]{1,0:T(8,128)(2,1)} %bitcast.54, bf16[2400,128]{1,0:T(8,128)(2,1)S(1)} %bitcast.73, bf16[2400,128]{1,0:T(8,128)(2,1)S(1)} %bitcast.72), kind=kOutput, calls=%fused_computation.1 | convolution fusion | flops 1260748800 | bytes 7192576 | tf_op jit(solution)/shard_map/dot_general | solution.py:37
  19.3 0.3 copy.16
  20.1 1.7 collective-permute-done
  21.9 10.1 %collective-permute-done.1 = bf16[64,2048]{0,1:T(8,128)(2,1)} collective-permute-done((bf16[64,2048]{0,1:T(8,128)(2,1)S(1)}, bf16[64,2048]{0,1:T(8,128)(2,1)}, u32[]{:S(2)}, u32[]{:S(2)}) %collective-permute-start.1) | collective-permute-done | bytes 262176 | tf_op jit(solution)/shard_map/ppermute | solution.py:95
  32.0 1.6 broadcast_select_fusion.1
  33.7 1.0 copy-done.1
  34.7 0.7 copy.27
  35.4 1.7 copy.28
  37.0 15.1 %all-to-all-start = ((bf16[128,32,128]{2,1,0:T(8,128)(2,1)}), bf16[128,32,128]{2,1,0:T(8,128)(2,1)S(1)}, u32[]{:S(2)}, u32[]{:S(2)}) async-start(bf16[128,32,128]{2,1,0:T(8,128)(2,1)} %copy.28), calls=%async_computation | async-start | bytes 2097152 | tf_op jit(solution)/shard_map/all_to_all | solution.py:114
  52.5 30.6 %all-to-all-done = bf16[128,32,128]{2,1,0:T(8,128)(2,1)S(1)} async-done(((bf16[128,32,128]{2,1,0:T(8,128)(2,1)}), bf16[128,32,128]{2,1,0:T(8,128)(2,1)S(1)}, u32[]{:S(2)}, u32[]{:S(2)}) %all-to-all-start) | async-done | bytes 1048608 | tf_op jit(solution)/shard_map/all_to_all | solution.py:114
  83.1 3.2 %gather_fusion = bf16[384,32,128]{2,1,0:T(8,128)(2,1)} fusion(bf16[128,32,128]{2,1,0:T(8,128)(2,1)S(1)} %all-to-all-done, s32[1024]{0:T(1024)S(1)} %pad_clamp_fusion), kind=kCustom, calls=%fused_computation | custom fusion | bytes 6292992 | tf_op jit(solution)/shard_map/jit(_take)/gather | solution.py:118
  86.3 7.0 %all-to-all-start.1 = ((bf16[128,96,128]{2,1,0:T(8,128)(2,1)}), bf16[128,96,128]{2,1,0:T(8,128)(2,1)S(1)}, u32[]{:S(2)}, u32[]{:S(2)}) async-start(bf16[128,96,128]{2,1,0:T(8,128)(2,1)} %bitcast.60), calls=%async_computation.1 | async-start | bytes 6291456 | tf_op jit(solution)/shard_map/all_to_all | solution.py:121
  93.3 7.3 %copy.26 = bf16[128,2,64,32]{3,2,1,0:T(8,128)(2,1)} copy(bf16[128,2,64,32]{0,3,1,2:T(8,128)(2,1)} %bitcast.63) | data formatting | bytes 2097152 | tf_op jit(solution)/shard_map/transpose | solution.py:110
  100.6 68.4 %all-to-all-done.1 = bf16[128,96,128]{2,1,0:T(8,128)(2,1)S(1)} async-done(((bf16[128,96,128]{2,1,0:T(8,128)(2,1)}), bf16[128,96,128]{2,1,0:T(8,128)(2,1)S(1)}, u32[]{:S(2)}, u32[]{:S(2)}) %all-to-all-start.1) | async-done | bytes 3145760 | tf_op jit(solution)/shard_map/all_to_all | solution.py:121
  169.0 1.7 copy-done
  170.7 7.9 %shard_map.28 = bf16[3,128,64,128]{3,2,1,0:T(8,128)(2,1)} custom-call(bf16[128,128,32]{2,1,0:T(8,128)(2,1)} %bitcast.55, bf16[128,3,32,128]{3,2,1,0:T(8,128)(2,1)} %bitcast.61), custom_call_target="tpu_custom_call" | custom-call | tf_op jit(solution)/shard_map/pallas_call | solution.py:70
  (32 shorter events, 3.1 us)
Async XLA Ops:
  6.9 15.0 %collective-permute-start = (bf16[64,2048]{0,1:T(8,128)(2,1)S(1)}, bf16[64,2048]{0,1:T(8,128)(2,1)}, u32[]{:S(2)}, u32[]{:S(2)}) collective-permute-start(bf16[64,2048]{0,1:T(8,128)(2,1)S(1)} %bitcast.74), channel_id=1, source_target_pairs={{0,1},{1,0},{2,3},{3,2},{4,5},{5,4},{6,7},{7,6},{8,9},{9,8},{10,11... | collective-permute-start | bytes 786440 | tf_op jit(solution)/shard_map/ppermute | solution.py:95
  14.1 17.9 %collective-permute-start.1 = (bf16[64,2048]{0,1:T(8,128)(2,1)S(1)}, bf16[64,2048]{0,1:T(8,128)(2,1)}, u32[]{:S(2)}, u32[]{:S(2)}) collective-permute-start(bf16[64,2048]{0,1:T(8,128)(2,1)S(1)} %bitcast.75), channel_id=1, source_target_pairs={{0,1},{1,0},{2,3},{3,2},{4,5},{5,4},{6,7},{7,6},{8,9},{9,8},{10,11... | collective-permute-start | bytes 786440 | tf_op jit(solution)/shard_map/ppermute | solution.py:95
  33.7 1.0 copy-start.1
  37.0 15.1 %copy-start.2 = (s32[3,128]{1,0:T(4,128)S(1)}, s32[3,128]{1,0:T(4,128)}, u32[]{:S(2)}) copy-start(s32[3,128]{1,0:T(4,128)} %param.3) | copy-start | bytes 4612
  37.0 46.1 %all-to-all-start = ((bf16[128,32,128]{2,1,0:T(8,128)(2,1)}), bf16[128,32,128]{2,1,0:T(8,128)(2,1)S(1)}, u32[]{:S(2)}, u32[]{:S(2)}) async-start(bf16[128,32,128]{2,1,0:T(8,128)(2,1)} %copy.28), calls=%async_computation | async-start | bytes 2097152 | tf_op jit(solution)/shard_map/all_to_all | solution.py:114
  86.3 82.8 %all-to-all-start.1 = ((bf16[128,96,128]{2,1,0:T(8,128)(2,1)}), bf16[128,96,128]{2,1,0:T(8,128)(2,1)S(1)}, u32[]{:S(2)}, u32[]{:S(2)}) async-start(bf16[128,96,128]{2,1,0:T(8,128)(2,1)} %bitcast.60), calls=%async_computation.1 | async-start | bytes 6291456 | tf_op jit(solution)/shard_map/all_to_all | solution.py:121
  169.0 1.7 copy-start

commit v10 on v9

--- a/solution.py
+++ b/solution.py
@@ -85,22 +85,27 @@
     n_grp = lax.axis_size("grp")
     g = lax.axis_index("grp")
     own_bins = F // n_grp
-    pieces = 2 if own_bins % 2 == 0 else 1
-    piece = own_bins // pieces
+    seg_total, chan_total = raw.shape[0], raw.shape[1]
+    pieces = 2 if chan_total % 2 == 0 else 1
+    piece = chan_total // pieces
+    kept = []
     received = []
     for i in range(pieces):
-        sent = whiten(raw, piece, (1 - g) * own_bins + i * piece)
-        half_ch, two, seg_count = sent.shape[1:]
+        spec = whiten(raw[:, i * piece:(i + 1) * piece], F, 0)
+        half_ch, two, seg_count = spec.shape[1:]
+        by_grp = spec.reshape(n_grp, own_bins, piece * two * seg_count)
+        kept.append(lax.dynamic_index_in_dim(by_grp, g, 0, keepdims=False))
         received.append(
             lax.ppermute(
-                sent.reshape(piece, half_ch * two * seg_count),
+                lax.dynamic_index_in_dim(by_grp, 1 - g, 0, keepdims=False),
                 "grp",
                 [(j, (j + 1) % n_grp) for j in range(n_grp)],
             )
         )
+    half_ch = chan_total
     norm_scale = 1.0 / math.sqrt(seg_count)
-    theirs = jnp.concatenate(received, axis=0)
-    mine = whiten(raw, own_bins, g * own_bins).reshape(own_bins, half_ch * two * seg_count)
+    mine = jnp.concatenate(kept, axis=1)
+    theirs = jnp.concatenate(received, axis=1)
     first = jnp.where(g == 0, mine, theirs)
     second = jnp.where(g == 0, theirs, mine)
     halves = jnp.stack([first, second], axis=1)

time: 179 us -> 172 us (0.961)
  matrix products: 13.1 us -> 3.03 us
  local copies, waits for them, and re-layouts: 17.1 us -> 22.4 us
  waiting for transfers between devices: 111 us -> 109 us
    dot_general x3 -> x2, matrix products: 13.1 us -> 3.03 us  [whiten(): jnp.dot(samples.reshape(seg_count * chan_count, length), dft_table(length...]
    dynamic_slice x0 -> x5, local copies, waits for them, and re-layouts: none -> 3.56 us  [the longest x3 2.86 us: per_device(): kept.append(lax.dynamic_index_in_dim(by_grp, g, 0, keepdims=False))]
    slice x0 -> x3, local copies, waits for them, and re-layouts: none -> 3.1 us  [the longest x1 2.82 us: per_device(): spec = whiten(raw[:, i * piece:(i + 1) * piece], F, 0)]
  transfers between devices with their start and end apart: 4 -> 4, of which waited for: 4 -> 4; matrix products, arithmetic and copies ran while one was open for 10% -> 5% of each run, Pallas kernels for 0% -> 0%
where the time goes in v10:
time: 172 us
  waiting for transfers between devices  109 us (63%)
  starting transfers between devices  24.4 us (14%)
  local copies, waits for them, and re-layouts  22.4 us (13%)
  Pallas kernels  7.91 us (5%)
  other arithmetic  4.47 us (3%)
  matrix products  3.03 us (2%)
    all_to_all x1, waiting for transfers between devices, per_device(): lax.all_to_all(gathered, 'blk', split_axis=0, concat_axis=0, tiled=True)  68.4 us
    all_to_all x1, waiting for transfers between devices, per_device(): lax.all_to_all(halves.reshape(n_blk, per_owner * seg_count, width), 'blk'...  30.6 us
    all_to_all x1, starting transfers between devices, per_device(): lax.all_to_all(halves.reshape(n_blk, per_owner * seg_count, width), 'blk'...  15 us
    ppermute x2, waiting for transfers between devices, per_device(): lax.ppermute(lax.dynamic_index_in_dim(by_grp, 1 - g, 0, keepdims=False),...  10.3 us
    pallas_call x1, Pallas kernels, cross(): pl.pallas_call(lambda *refs: cross_kernel(scale, *refs), grid=(own_bins /...  7.91 us
    transpose x1, local copies, waits for them, and re-layouts, per_device(): jnp.transpose(halves, (0, 2, 1, 3))  7.28 us
    all_to_all x1, starting transfers between devices, per_device(): lax.all_to_all(gathered, 'blk', split_axis=0, concat_axis=0, tiled=True)  7.04 us
  transfers between devices with their start and end apart: 4, of which 4 were waited for; matrix products, arithmetic and copies ran while one was open for 5% of the time, Pallas kernels for 0%

profile of v10, /device:TPU:32, one launch (start us, length us, event | category | flops | bytes accessed | tf_op | source)
XLA Modules:
  0.0 171.8 jit_solution(4445766224918761566)
XLA Ops:
  0.6 2.8 %fusion.22 = (bf16[32,16,2400]{2,1,0:T(8,128)(2,1)S(1)}, bf16[32,16,2400]{2,1,0:T(8,128)(2,1)S(1)}) fusion(bf16[32,32,2400]{2,1,0:T(8,128)(2,1)} %param.2), kind=kLoop, calls=%fused_computation.52 | loop fusion | bytes 9830400 | tf_op jit(solution)/shard_map/slice | solution.py:94
  3.4 1.1 subtract_convert_fusion
  4.5 1.5 fusion
  6.0 1.5 fusion.1
  7.9 0.6 add_reduce_fusion.1
  8.5 0.6 fusion.2
  9.3 0.6 add_reduce_fusion
  9.9 0.6 fusion.4
  10.6 2.2 %constant_dynamic-slice_fusion.2 = (bf16[1,128,1024]{1,0,2:T(2,128)(2,1)S(1)}, bf16[1,128,1024]{1,0,2:T(2,128)(2,1)S(1)}, bf16[1,128,1024]{1,0,2:T(2,128)(2,1)S(1)}, bf16[1,128,1024]{1,0,2:T(2,128)(2,1)S(1)}) fusion(bf16[2,128,1024]{1,0,2:T(2,128)(2,1)S(1)} %reshape.271, s32[]{:T(128)S(6)} %select_n.73, s32[]{:T(128)S(6)} %select_n.74, ...), kind=kLoop, calls=%fused_computation.47 | loop fusion | bytes 2097160 | tf_op jit(solution)/shard_map/jit(dynamic_index_in_dim)/dynamic_slice | solution.py:97
  13.2 1.7 collective-permute-start
  15.2 0.7 collective-permute-start.1
  16.6 5.8 %collective-permute-done = bf16[128,1024]{1,0:T(8,128)(2,1)S(1)} collective-permute-done((bf16[128,1024]{1,0:T(8,128)(2,1)S(1)}, bf16[128,1024]{1,0:T(8,128)(2,1)S(1)}, u32[]{:S(2)}, u32[]{:S(2)}) %collective-permute-start) | collective-permute-done | bytes 262176 | tf_op jit(solution)/shard_map/ppermute | solution.py:99
  22.4 4.5 %collective-permute-done.1 = bf16[128,1024]{1,0:T(8,128)(2,1)S(1)} collective-permute-done((bf16[128,1024]{1,0:T(8,128)(2,1)S(1)}, bf16[128,1024]{1,0:T(8,128)(2,1)S(1)}, u32[]{:S(2)}, u32[]{:S(2)}) %collective-permute-start.1) | collective-permute-done | bytes 262176 | tf_op jit(solution)/shard_map/ppermute | solution.py:99
  27.3 0.7 copy.25
  27.9 0.7 copy.27
  28.6 1.7 copy.28
  30.3 15.0 %all-to-all-start = ((bf16[128,32,128]{2,1,0:T(8,128)(2,1)}), bf16[128,32,128]{2,1,0:T(8,128)(2,1)S(1)}, u32[]{:S(2)}, u32[]{:S(2)}) async-start(bf16[128,32,128]{2,1,0:T(8,128)(2,1)} %copy.28), calls=%async_computation | async-start | bytes 2097152 | tf_op jit(solution)/shard_map/all_to_all | solution.py:119
  45.7 30.6 %all-to-all-done = bf16[128,32,128]{2,1,0:T(8,128)(2,1)S(1)} async-done(((bf16[128,32,128]{2,1,0:T(8,128)(2,1)}), bf16[128,32,128]{2,1,0:T(8,128)(2,1)S(1)}, u32[]{:S(2)}, u32[]{:S(2)}) %all-to-all-start) | async-done | bytes 1048608 | tf_op jit(solution)/shard_map/all_to_all | solution.py:119
  76.3 3.2 %gather_fusion = bf16[384,32,128]{2,1,0:T(8,128)(2,1)} fusion(bf16[128,32,128]{2,1,0:T(8,128)(2,1)S(1)} %all-to-all-done, s32[1024]{0:T(1024)S(1)} %pad_clamp_fusion), kind=kCustom, calls=%fused_computation | custom fusion | bytes 6292992 | tf_op jit(solution)/shard_map/jit(_take)/gather | solution.py:123
  79.4 7.0 %all-to-all-start.1 = ((bf16[128,96,128]{2,1,0:T(8,128)(2,1)}), bf16[128,96,128]{2,1,0:T(8,128)(2,1)S(1)}, u32[]{:S(2)}, u32[]{:S(2)}) async-start(bf16[128,96,128]{2,1,0:T(8,128)(2,1)} %bitcast.53), calls=%async_computation.1 | async-start | bytes 6291456 | tf_op jit(solution)/shard_map/all_to_all | solution.py:126
  86.5 7.3 %copy.26 = bf16[128,2,64,32]{3,2,1,0:T(8,128)(2,1)} copy(bf16[128,2,64,32]{0,3,1,2:T(8,128)(2,1)} %bitcast.56) | data formatting | bytes 2097152 | tf_op jit(solution)/shard_map/transpose | solution.py:115
  93.8 68.4 %all-to-all-done.1 = bf16[128,96,128]{2,1,0:T(8,128)(2,1)S(1)} async-done(((bf16[128,96,128]{2,1,0:T(8,128)(2,1)}), bf16[128,96,128]{2,1,0:T(8,128)(2,1)S(1)}, u32[]{:S(2)}, u32[]{:S(2)}) %all-to-all-start.1) | async-done | bytes 3145760 | tf_op jit(solution)/shard_map/all_to_all | solution.py:126
  162.2 1.7 copy-done
  163.9 7.9 %shard_map.28 = bf16[3,128,64,128]{3,2,1,0:T(8,128)(2,1)} custom-call(bf16[128,128,32]{2,1,0:T(8,128)(2,1)} %bitcast.52, bf16[128,3,32,128]{3,2,1,0:T(8,128)(2,1)} %bitcast.54), custom_call_target="tpu_custom_call" | custom-call | tf_op jit(solution)/shard_map/pallas_call | solution.py:70
  (26 shorter events, 3.3 us)
Async XLA Ops:
  13.2 9.3 %collective-permute-start = (bf16[128,1024]{1,0:T(8,128)(2,1)S(1)}, bf16[128,1024]{1,0:T(8,128)(2,1)S(1)}, u32[]{:S(2)}, u32[]{:S(2)}) collective-permute-start(bf16[128,1024]{1,0:T(8,128)(2,1)S(1)} %bitcast.70), channel_id=1, source_target_pairs={{0,1},{1,0},{2,3},{3,2},{4,5},{5,4},{6,7},{7,6},{8,9},{9,8},{10,11... | collective-permute-start | bytes 786440 | tf_op jit(solution)/shard_map/ppermute | solution.py:99
  15.2 11.7 %collective-permute-start.1 = (bf16[128,1024]{1,0:T(8,128)(2,1)S(1)}, bf16[128,1024]{1,0:T(8,128)(2,1)S(1)}, u32[]{:S(2)}, u32[]{:S(2)}) collective-permute-start(bf16[128,1024]{1,0:T(8,128)(2,1)S(1)} %bitcast.71), channel_id=1, source_target_pairs={{0,1},{1,0},{2,3},{3,2},{4,5},{5,4},{6,7},{7,6},{8,9},{9,8},{10,11... | collective-permute-start | bytes 786440 | tf_op jit(solution)/shard_map/ppermute | solution.py:99
  27.9 2.4 %copy-start.1 = (bf16[128,2,2048]{0,2,1:T(8,128)(2,1)}, bf16[128,2,2048]{0,2,1:T(8,128)(2,1)S(1)}, u32[]{:S(2)}) copy-start(bf16[128,2,2048]{0,2,1:T(8,128)(2,1)S(1)} %copy.25) | copy-start | bytes 3145732
  28.6 16.7 %copy-start.2 = (s32[3,128]{1,0:T(4,128)S(1)}, s32[3,128]{1,0:T(4,128)}, u32[]{:S(2)}) copy-start(s32[3,128]{1,0:T(4,128)} %param.3) | copy-start | bytes 4612
  30.3 46.0 %all-to-all-start = ((bf16[128,32,128]{2,1,0:T(8,128)(2,1)}), bf16[128,32,128]{2,1,0:T(8,128)(2,1)S(1)}, u32[]{:S(2)}, u32[]{:S(2)}) async-start(bf16[128,32,128]{2,1,0:T(8,128)(2,1)} %copy.28), calls=%async_computation | async-start | bytes 2097152 | tf_op jit(solution)/shard_map/all_to_all | solution.py:119
  79.4 82.8 %all-to-all-start.1 = ((bf16[128,96,128]{2,1,0:T(8,128)(2,1)}), bf16[128,96,128]{2,1,0:T(8,128)(2,1)S(1)}, u32[]{:S(2)}, u32[]{:S(2)}) async-start(bf16[128,96,128]{2,1,0:T(8,128)(2,1)} %bitcast.53), calls=%async_computation.1 | async-start | bytes 6291456 | tf_op jit(solution)/shard_map/all_to_all | solution.py:126
  162.2 1.7 copy-start

commit v11 on v8

--- a/solution.py
+++ b/solution.py
@@ -97,15 +97,22 @@
     first = jnp.where(g == 0, mine, theirs)
     second = jnp.where(g == 0, theirs, mine)
     halves = jnp.stack([first, second], axis=1)
-    own_bins = halves.shape[0]
     block_ch = n_grp * half_ch
     halves = halves.reshape(own_bins, block_ch, two, seg_count)
     own = jnp.transpose(halves, (0, 2, 1, 3)).reshape(own_bins, two * block_ch, seg_count)
-    halves = jnp.transpose(halves, (0, 3, 2, 1))
     width = two * block_ch
     per_owner = own_bins // n_blk
+
+    def seg_major(x):
+        return jnp.transpose(x.reshape(own_bins, half_ch, two, seg_count), (0, 3, 2, 1))
+
+    rec_mine = seg_major(mine)
+    rec_theirs = seg_major(theirs)
+    rec = jnp.where(
+        g == 0, jnp.stack([rec_mine, rec_theirs], axis=3), jnp.stack([rec_theirs, rec_mine], axis=3)
+    )
     owned = lax.all_to_all(
-        halves.reshape(n_blk, per_owner * seg_count, width), "blk", split_axis=0, concat_axis=0, tiled=True
+        rec.reshape(n_blk, per_owner * seg_count, width), "blk", split_axis=0, concat_axis=0, tiled=True
     )
     rounds = partner.shape[0]
     gathered = jnp.take(owned, jnp.transpose(partner).reshape(-1), axis=0, mode="clip")

time: 167 us -> 166 us (level)
  waiting for transfers between devices: 107 us -> 103 us
  other arithmetic: 2.99 us -> 4.75 us
    all_to_all x1, waiting for transfers between devices: 68.4 us -> 65.9 us  [per_device(): lax.all_to_all(gathered, 'blk', split_axis=0, concat_axis=0, tiled=True)]
    select_n x0 -> x2, local copies, waits for them, and re-layouts: none -> 1.79 us  [per_device(): jnp.where(g == 0, jnp.stack([rec_mine, rec_theirs], axis=3), jnp.stack([r...]
    another operation x1 -> x2, other arithmetic: 0.73 us -> 2.42 us
  transfers between devices with their start and end apart: 3 -> 3, of which waited for: 3 -> 3; matrix products, arithmetic and copies ran while one was open for 7% -> 9% of each run, Pallas kernels for 0% -> 0%
where the time goes in v11:
time: 166 us
  waiting for transfers between devices  103 us (62%)
  starting transfers between devices  23.8 us (14%)
  local copies, waits for them, and re-layouts  17.9 us (11%)
  matrix products  7.98 us (5%)
  Pallas kernels  7.91 us (5%)
  other arithmetic  4.75 us (3%)
    all_to_all x1, waiting for transfers between devices, per_device(): lax.all_to_all(gathered, 'blk', split_axis=0, concat_axis=0, tiled=True)  65.9 us
    all_to_all x1, waiting for transfers between devices, per_device(): lax.all_to_all(rec.reshape(n_blk, per_owner * seg_count, width), 'blk', s...  30.6 us
    all_to_all x1, starting transfers between devices, per_device(): lax.all_to_all(rec.reshape(n_blk, per_owner * seg_count, width), 'blk', s...  15.1 us
    dot_general x2, matrix products, whiten(): jnp.dot(samples.reshape(seg_count * chan_count, length), dft_table(length...  7.98 us
    pallas_call x1, Pallas kernels, cross(): pl.pallas_call(lambda *refs: cross_kernel(scale, *refs), grid=(own_bins /...  7.91 us
    transpose x1, local copies, waits for them, and re-layouts, per_device(): jnp.transpose(halves, (0, 2, 1, 3))  7.31 us
    all_to_all x1, starting transfers between devices, per_device(): lax.all_to_all(gathered, 'blk', split_axis=0, concat_axis=0, tiled=True)  7.05 us
    ppermute x1, waiting for transfers between devices, per_device(): lax.ppermute(sent.reshape(own_bins, half_ch * two * seg_count), 'grp', [(...  6.88 us
  transfers between devices with their start and end apart: 3, of which 3 were waited for; matrix products, arithmetic and copies ran while one was open for 9% of the time, Pallas kernels for 0%

profile of v11, /device:TPU:32, one launch (start us, length us, event | category | flops | bytes accessed | tf_op | source)
XLA Modules:
  0.0 165.8 jit_solution(5392147241899078247)
XLA Ops:
  0.3 0.3 fusion.21
  0.6 1.5 subtract_convert_fusion
  2.1 4.0 %convolution_bitcast_fusion = f32[1024,256]{0,1:T(8,128)S(1)} fusion(bf16[1024,2400]{1,0:T(8,128)(2,1)} %bitcast.67, bf16[2400,128]{1,0:T(8,128)(2,1)S(1)} %bitcast.65, bf16[2400,128]{1,0:T(8,128)(2,1)S(1)} %bitcast.64), kind=kOutput, calls=%fused_computation.1 | convolution fusion | flops 1260748800 | bytes 7192576 | tf_op jit(solution)/shard_map/dot_general | solution.py:37
  6.1 0.3 copy.13
  6.8 1.0 copy.14
  7.8 1.6 collective-permute-start
  9.3 4.0 %convolution_bitcast_fusion.1 = f32[1024,256]{0,1:T(8,128)S(1)} fusion(bf16[1024,2400]{1,0:T(8,128)(2,1)} %bitcast.68, bf16[2400,128]{1,0:T(8,128)(2,1)S(1)} %bitcast.62, bf16[2400,128]{1,0:T(8,128)(2,1)S(1)} %bitcast.63), kind=kOutput, calls=%fused_computation.2 | convolution fusion | flops 1260748800 | bytes 7192576 | tf_op jit(solution)/shard_map/dot_general | solution.py:37
  13.3 0.3 copy.11
  13.9 0.9 fusion.8
  14.7 6.9 %collective-permute-done = bf16[128,2048]{0,1:T(8,128)(2,1)S(1)} collective-permute-done((bf16[128,2048]{0,1:T(8,128)(2,1)}, bf16[128,2048]{0,1:T(8,128)(2,1)S(1)}, u32[]{:S(2)}, u32[]{:S(2)}) %collective-permute-start) | collective-permute-done | bytes 524320 | tf_op jit(solution)/shard_map/ppermute | solution.py:91
  21.6 0.3 copy.21
  22.2 0.3 copy-done.1
  22.5 1.7 %copy.18 = bf16[128,32,128]{2,1,0:T(8,128)(2,1)} copy(bf16[128,32,128]{0,2,1:T(8,128)(2,1)S(1)} %bitcast.57) | data formatting | bytes 2097152 | tf_op jit(solution)/shard_map/jit(_where)/select_n | solution.py:111
  24.2 15.1 %all-to-all-start = ((bf16[128,32,128]{2,1,0:T(8,128)(2,1)}), bf16[128,32,128]{2,1,0:T(8,128)(2,1)S(1)}, u32[]{:S(2)}, u32[]{:S(2)}) async-start(bf16[128,32,128]{2,1,0:T(8,128)(2,1)} %copy.18), calls=%async_computation | async-start | bytes 2097152 | tf_op jit(solution)/shard_map/all_to_all | solution.py:114
  39.5 0.2 reshape.274
  39.7 30.6 %all-to-all-done = bf16[128,32,128]{2,1,0:T(8,128)(2,1)S(1)} async-done(((bf16[128,32,128]{2,1,0:T(8,128)(2,1)}), bf16[128,32,128]{2,1,0:T(8,128)(2,1)S(1)}, u32[]{:S(2)}, u32[]{:S(2)}) %all-to-all-start) | async-done | bytes 1048608 | tf_op jit(solution)/shard_map/all_to_all | solution.py:114
  70.3 3.2 %gather_fusion = bf16[384,32,128]{2,1,0:T(8,128)(2,1)} fusion(bf16[128,32,128]{2,1,0:T(8,128)(2,1)S(1)} %all-to-all-done, s32[1024]{0:T(1024)S(1)} %pad_clamp_fusion), kind=kCustom, calls=%fused_computation | custom fusion | bytes 6292992 | tf_op jit(solution)/shard_map/jit(_take)/gather | solution.py:118
  73.5 7.1 %all-to-all-start.1 = ((bf16[128,96,128]{2,1,0:T(8,128)(2,1)}), bf16[128,96,128]{2,1,0:T(8,128)(2,1)S(1)}, u32[]{:S(2)}, u32[]{:S(2)}) async-start(bf16[128,96,128]{2,1,0:T(8,128)(2,1)} %bitcast.50), calls=%async_computation.1 | async-start | bytes 6291456 | tf_op jit(solution)/shard_map/all_to_all | solution.py:121
  80.6 1.3 copy.12
  82.0 1.1 pad_maximum_fusion
  83.0 7.3 %copy.15 = bf16[128,2,64,32]{3,2,1,0:T(8,128)(2,1)} copy(bf16[128,2,64,32]{0,3,1,2:T(8,128)(2,1)} %bitcast.56) | data formatting | bytes 2097152 | tf_op jit(solution)/shard_map/transpose | solution.py:102
  90.3 65.9 %all-to-all-done.1 = bf16[128,96,128]{2,1,0:T(8,128)(2,1)S(1)} async-done(((bf16[128,96,128]{2,1,0:T(8,128)(2,1)}), bf16[128,96,128]{2,1,0:T(8,128)(2,1)S(1)}, u32[]{:S(2)}, u32[]{:S(2)}) %all-to-all-start.1) | async-done | bytes 3145760 | tf_op jit(solution)/shard_map/all_to_all | solution.py:121
  156.2 1.7 %copy-done = bf16[128,96,128]{2,1,0:T(8,128)(2,1)} copy-done((bf16[128,96,128]{2,1,0:T(8,128)(2,1)}, bf16[128,96,128]{2,1,0:T(8,128)(2,1)S(1)}, u32[]{:S(2)}) %copy-start) | copy-done | bytes 3145752
  157.9 7.9 %shard_map.28 = bf16[3,128,64,128]{3,2,1,0:T(8,128)(2,1)} custom-call(bf16[128,128,32]{2,1,0:T(8,128)(2,1)} %bitcast.49, bf16[128,3,32,128]{3,2,1,0:T(8,128)(2,1)} %bitcast.51), custom_call_target="tpu_custom_call" | custom-call | tf_op jit(solution)/shard_map/pallas_call | solution.py:70
  (25 shorter events, 1.2 us)
Async XLA Ops:
  6.7 2.7 %copy-start.3 = (bf16[50,48,128]{2,1,0:T(8,128)(2,1)S(1)}, bf16[50,48,128]{2,1,0:T(8,128)(2,1)}, u32[]{:S(2)}) copy-start(bf16[50,48,128]{2,1,0:T(8,128)(2,1)} %get-tuple-element.28) | copy-start | bytes 1843204
  7.8 13.9 %collective-permute-start = (bf16[128,2048]{0,1:T(8,128)(2,1)}, bf16[128,2048]{0,1:T(8,128)(2,1)S(1)}, u32[]{:S(2)}, u32[]{:S(2)}) collective-permute-start(bf16[128,2048]{0,1:T(8,128)(2,1)} %bitcast.16), channel_id=1, source_target_pairs={{0,1},{1,0},{2,3},{3,2},{4,5},{5,4},{6,7},{7,6},{8,9},{9,8},{10,11... | collective-permute-start | bytes 1572872 | tf_op jit(solution)/shard_map/ppermute | solution.py:91
  21.6 0.8 copy-start.1
  24.2 15.1 %copy-start.4 = (s32[3,128]{1,0:T(4,128)S(1)}, s32[3,128]{1,0:T(4,128)}, u32[]{:S(2)}) copy-start(s32[3,128]{1,0:T(4,128)} %param.3) | copy-start | bytes 4612
  24.2 46.1 %all-to-all-start = ((bf16[128,32,128]{2,1,0:T(8,128)(2,1)}), bf16[128,32,128]{2,1,0:T(8,128)(2,1)S(1)}, u32[]{:S(2)}, u32[]{:S(2)}) async-start(bf16[128,32,128]{2,1,0:T(8,128)(2,1)} %copy.18), calls=%async_computation | async-start | bytes 2097152 | tf_op jit(solution)/shard_map/all_to_all | solution.py:114
  73.5 82.8 %all-to-all-start.1 = ((bf16[128,96,128]{2,1,0:T(8,128)(2,1)}), bf16[128,96,128]{2,1,0:T(8,128)(2,1)S(1)}, u32[]{:S(2)}, u32[]{:S(2)}) async-start(bf16[128,96,128]{2,1,0:T(8,128)(2,1)} %bitcast.50), calls=%async_computation.1 | async-start | bytes 6291456 | tf_op jit(solution)/shard_map/all_to_all | solution.py:121
  80.5 1.3 copy-start.2
  156.2 1.7 %copy-start = (bf16[128,96,128]{2,1,0:T(8,128)(2,1)}, bf16[128,96,128]{2,1,0:T(8,128)(2,1)S(1)}, u32[]{:S(2)}) copy-start(bf16[128,96,128]{2,1,0:T(8,128)(2,1)S(1)} %all-to-all-done.1) | copy-start | bytes 9437188

commit v12 on v11

--- a/solution.py
+++ b/solution.py
@@ -66,7 +66,7 @@
     own_bins, two_ch, seg_count = a.shape
     rounds, width = rec.shape[1], rec.shape[-1]
     block_ch = two_ch // 2
-    fb = 32
+    fb = 16
     return pl.pallas_call(
         lambda *refs: cross_kernel(scale, *refs),
         grid=(own_bins // fb,),

time: 166 us -> 168 us (1.012)
  Pallas kernels: 7.91 us -> 9.72 us
    pallas_call x1, Pallas kernels: 7.91 us -> 9.72 us  [cross(): pl.pallas_call(lambda *refs: cross_kernel(scale, *refs), grid=(own_bins /...]
where the time goes in v12:
time: 168 us
  waiting for transfers between devices  103 us (61%)
  starting transfers between devices  23.8 us (14%)
  local copies, waits for them, and re-layouts  17.9 us (11%)
  Pallas kernels  9.72 us (6%)
  matrix products  7.99 us (5%)
  other arithmetic  4.75 us (3%)
    all_to_all x1, waiting for transfers between devices, per_device(): lax.all_to_all(gathered, 'blk', split_axis=0, concat_axis=0, tiled=True)  65.9 us
    all_to_all x1, waiting for transfers between devices, per_device(): lax.all_to_all(rec.reshape(n_blk, per_owner * seg_count, width), 'blk', s...  30.6 us
    all_to_all x1, starting transfers between devices, per_device(): lax.all_to_all(rec.reshape(n_blk, per_owner * seg_count, width), 'blk', s...  15.1 us
    pallas_call x1, Pallas kernels, cross(): pl.pallas_call(lambda *refs: cross_kernel(scale, *refs), grid=(own_bins /...  9.72 us
    dot_general x2, matrix products, whiten(): jnp.dot(samples.reshape(seg_count * chan_count, length), dft_table(length...  7.99 us
    transpose x1, local copies, waits for them, and re-layouts, per_device(): jnp.transpose(halves, (0, 2, 1, 3))  7.31 us
    all_to_all x1, starting transfers between devices, per_device(): lax.all_to_all(gathered, 'blk', split_axis=0, concat_axis=0, tiled=True)  7.04 us
    ppermute x1, waiting for transfers between devices, per_device(): lax.ppermute(sent.reshape(own_bins, half_ch * two * seg_count), 'grp', [(...  6.87 us
  transfers between devices with their start and end apart: 3, of which 3 were waited for; matrix products, arithmetic and copies ran while one was open for 9% of the time, Pallas kernels for 0%

profile of v12, /device:TPU:32, one launch (start us, length us, event | category | flops | bytes accessed | tf_op | source)
XLA Modules:
  0.0 167.6 jit_solution(16287602324108822456)
XLA Ops:
  0.3 0.3 fusion.21
  0.6 1.5 subtract_convert_fusion
  2.1 4.0 %convolution_bitcast_fusion = f32[1024,256]{0,1:T(8,128)S(1)} fusion(bf16[1024,2400]{1,0:T(8,128)(2,1)} %bitcast.67, bf16[2400,128]{1,0:T(8,128)(2,1)S(1)} %bitcast.65, bf16[2400,128]{1,0:T(8,128)(2,1)S(1)} %bitcast.64), kind=kOutput, calls=%fused_computation.1 | convolution fusion | flops 1260748800 | bytes 7192576 | tf_op jit(solution)/shard_map/dot_general | solution.py:37
  6.1 0.3 copy.13
  6.7 1.0 copy.14
  7.8 1.6 collective-permute-start
  9.3 4.0 %convolution_bitcast_fusion.1 = f32[1024,256]{0,1:T(8,128)S(1)} fusion(bf16[1024,2400]{1,0:T(8,128)(2,1)} %bitcast.68, bf16[2400,128]{1,0:T(8,128)(2,1)S(1)} %bitcast.62, bf16[2400,128]{1,0:T(8,128)(2,1)S(1)} %bitcast.63), kind=kOutput, calls=%fused_computation.2 | convolution fusion | flops 1260748800 | bytes 7192576 | tf_op jit(solution)/shard_map/dot_general | solution.py:37
  13.3 0.3 copy.11
  13.9 0.9 fusion.8
  14.8 6.9 %collective-permute-done = bf16[128,2048]{0,1:T(8,128)(2,1)S(1)} collective-permute-done((bf16[128,2048]{0,1:T(8,128)(2,1)}, bf16[128,2048]{0,1:T(8,128)(2,1)S(1)}, u32[]{:S(2)}, u32[]{:S(2)}) %collective-permute-start) | collective-permute-done | bytes 524320 | tf_op jit(solution)/shard_map/ppermute | solution.py:91
  21.6 0.3 copy.21
  22.2 0.3 copy-done.1
  22.5 1.7 copy.18
  24.2 15.1 %all-to-all-start = ((bf16[128,32,128]{2,1,0:T(8,128)(2,1)}), bf16[128,32,128]{2,1,0:T(8,128)(2,1)S(1)}, u32[]{:S(2)}, u32[]{:S(2)}) async-start(bf16[128,32,128]{2,1,0:T(8,128)(2,1)} %copy.18), calls=%async_computation | async-start | bytes 2097152 | tf_op jit(solution)/shard_map/all_to_all | solution.py:114
  39.5 0.2 reshape.274
  39.7 30.6 %all-to-all-done = bf16[128,32,128]{2,1,0:T(8,128)(2,1)S(1)} async-done(((bf16[128,32,128]{2,1,0:T(8,128)(2,1)}), bf16[128,32,128]{2,1,0:T(8,128)(2,1)S(1)}, u32[]{:S(2)}, u32[]{:S(2)}) %all-to-all-start) | async-done | bytes 1048608 | tf_op jit(solution)/shard_map/all_to_all | solution.py:114
  70.3 3.2 %gather_fusion = bf16[384,32,128]{2,1,0:T(8,128)(2,1)} fusion(bf16[128,32,128]{2,1,0:T(8,128)(2,1)S(1)} %all-to-all-done, s32[1024]{0:T(1024)S(1)} %pad_clamp_fusion), kind=kCustom, calls=%fused_computation | custom fusion | bytes 6292992 | tf_op jit(solution)/shard_map/jit(_take)/gather | solution.py:118
  73.5 7.0 %all-to-all-start.1 = ((bf16[128,96,128]{2,1,0:T(8,128)(2,1)}), bf16[128,96,128]{2,1,0:T(8,128)(2,1)S(1)}, u32[]{:S(2)}, u32[]{:S(2)}) async-start(bf16[128,96,128]{2,1,0:T(8,128)(2,1)} %bitcast.50), calls=%async_computation.1 | async-start | bytes 6291456 | tf_op jit(solution)/shard_map/all_to_all | solution.py:121
  80.5 1.3 copy.12
  82.0 1.1 pad_maximum_fusion
  83.0 7.3 %copy.15 = bf16[128,2,64,32]{3,2,1,0:T(8,128)(2,1)} copy(bf16[128,2,64,32]{0,3,1,2:T(8,128)(2,1)} %bitcast.56) | data formatting | bytes 2097152 | tf_op jit(solution)/shard_map/transpose | solution.py:102
  90.3 65.9 %all-to-all-done.1 = bf16[128,96,128]{2,1,0:T(8,128)(2,1)S(1)} async-done(((bf16[128,96,128]{2,1,0:T(8,128)(2,1)}), bf16[128,96,128]{2,1,0:T(8,128)(2,1)S(1)}, u32[]{:S(2)}, u32[]{:S(2)}) %all-to-all-start.1) | async-done | bytes 3145760 | tf_op jit(solution)/shard_map/all_to_all | solution.py:121
  156.2 1.7 %copy-done = bf16[128,96,128]{2,1,0:T(8,128)(2,1)} copy-done((bf16[128,96,128]{2,1,0:T(8,128)(2,1)}, bf16[128,96,128]{2,1,0:T(8,128)(2,1)S(1)}, u32[]{:S(2)}) %copy-start) | copy-done | bytes 3145752
  157.9 9.7 %shard_map.28 = bf16[3,128,64,128]{3,2,1,0:T(8,128)(2,1)} custom-call(bf16[128,128,32]{2,1,0:T(8,128)(2,1)} %bitcast.49, bf16[128,3,32,128]{3,2,1,0:T(8,128)(2,1)} %bitcast.51), custom_call_target="tpu_custom_call" | custom-call | tf_op jit(solution)/shard_map/pallas_call | solution.py:70
  (25 shorter events, 1.2 us)
Async XLA Ops:
  6.7 2.7 %copy-start.3 = (bf16[50,48,128]{2,1,0:T(8,128)(2,1)S(1)}, bf16[50,48,128]{2,1,0:T(8,128)(2,1)}, u32[]{:S(2)}) copy-start(bf16[50,48,128]{2,1,0:T(8,128)(2,1)} %get-tuple-element.28) | copy-start | bytes 1843204
  7.8 13.9 %collective-permute-start = (bf16[128,2048]{0,1:T(8,128)(2,1)}, bf16[128,2048]{0,1:T(8,128)(2,1)S(1)}, u32[]{:S(2)}, u32[]{:S(2)}) collective-permute-start(bf16[128,2048]{0,1:T(8,128)(2,1)} %bitcast.16), channel_id=1, source_target_pairs={{0,1},{1,0},{2,3},{3,2},{4,5},{5,4},{6,7},{7,6},{8,9},{9,8},{10,11... | collective-permute-start | bytes 1572872 | tf_op jit(solution)/shard_map/ppermute | solution.py:91
  21.6 0.8 copy-start.1
  24.2 15.2 %copy-start.4 = (s32[3,128]{1,0:T(4,128)S(1)}, s32[3,128]{1,0:T(4,128)}, u32[]{:S(2)}) copy-start(s32[3,128]{1,0:T(4,128)} %param.3) | copy-start | bytes 4612
  24.2 46.1 %all-to-all-start = ((bf16[128,32,128]{2,1,0:T(8,128)(2,1)}), bf16[128,32,128]{2,1,0:T(8,128)(2,1)S(1)}, u32[]{:S(2)}, u32[]{:S(2)}) async-start(bf16[128,32,128]{2,1,0:T(8,128)(2,1)} %copy.18), calls=%async_computation | async-start | bytes 2097152 | tf_op jit(solution)/shard_map/all_to_all | solution.py:114
  73.5 82.8 %all-to-all-start.1 = ((bf16[128,96,128]{2,1,0:T(8,128)(2,1)}), bf16[128,96,128]{2,1,0:T(8,128)(2,1)S(1)}, u32[]{:S(2)}, u32[]{:S(2)}) async-start(bf16[128,96,128]{2,1,0:T(8,128)(2,1)} %bitcast.50), calls=%async_computation.1 | async-start | bytes 6291456 | tf_op jit(solution)/shard_map/all_to_all | solution.py:121
  80.5 1.3 copy-start.2
  156.2 1.7 %copy-start = (bf16[128,96,128]{2,1,0:T(8,128)(2,1)}, bf16[128,96,128]{2,1,0:T(8,128)(2,1)S(1)}, u32[]{:S(2)}) copy-start(bf16[128,96,128]{2,1,0:T(8,128)(2,1)S(1)} %all-to-all-done.1) | copy-start | bytes 9437188
